TPU v7x, 128 devices: a whole 4x4x4 slice. The times are simulated.
128 devices in a mesh: node: 8 (over z, core), local: 16 (over x, y).
Axes of the slice: x: 4, y: 4, z: 4, core: 2. Of those that a mesh axis runs over, the one named last changes fastest.
Arguments:
- tokens: bfloat16 [16384, 4096], P(('node', 'local')), may hold values from -6 to 6
- cotangent: bfloat16 [16384, 4096], P(('node', 'local')), may hold values from -6 to 6
- gate_probs: float32 [16384, 8], P(('node', 'local')), may hold values from 0.02 to 0.5
- experts: int32 [16384, 8], P(('node', 'local')), may hold values from 0 to 127, all different within a row; in each aligned block of 128 rows (0 to 127, 128 to 255, ...) at most 10 rows name the same one
- stratum: int32 [128], P(('node', 'local')), may hold values from 0 to 7
- token_level: int32 [16384], P(('node', 'local')), may hold values from 0 to 63
- w_gate_up: bfloat16 [128, 4096, 1024], P(('node', 'local')), may hold values from -0.09375 to 0.09375
- w_down: bfloat16 [128, 512, 4096], P(('node', 'local')), may hold values from -0.25 to 0.25
Outputs:
- grad_tokens: bfloat16 [16384, 4096], P(('node', 'local'))
- grad_probs: bfloat16 [16384, 8], P(('node', 'local'))
Inputs may be any that keep to these rules, and one draw needn't show every extreme that they name: Among the tokens of one device no expert is named more than 10 times; in every draw some expert is named exactly 10 times by the tokens of some device. A token names 8 different experts.
All inputs are finite; a program needn't handle non-finite values.
Results may differ from a plain program's by a relative error of at most 0.013.
Values may be sent and summed in bfloat16 or wider, within the bound.
No kernel may reach another device: no remote copies, remote signals or barrier semaphores. Data moves between devices by JAX's collectives and lax.ppermute only.
A program may use at most 192 MiB of HBM per device.

v0:
```python
import jax
import jax.numpy as jnp
from jax import lax
from jax.sharding import PartitionSpec as P

STRATA = 8
LEVELS = 64
CHUNK_SIZES = (3, 4, 3)


def expert_grads(inputs, upstream, weight_in, weight_out):
    hidden_units = weight_out.shape[0]
    projected = jnp.dot(inputs, weight_in, preferred_element_type=jnp.float32)
    gate_part = projected[:, :hidden_units]
    up_part = projected[:, hidden_units:]
    sigmoid_gate = jax.nn.sigmoid(gate_part)
    activated = gate_part * sigmoid_gate
    hidden = (activated * up_part).astype(jnp.bfloat16)
    backward = jnp.dot(upstream, weight_out.T, preferred_element_type=jnp.float32)
    prob_grad = jnp.sum(hidden.astype(jnp.float32) * backward, axis=1).astype(jnp.bfloat16)
    grad_gate = backward * up_part * sigmoid_gate * (1.0 + gate_part * (1.0 - sigmoid_gate))
    grad_up = backward * activated
    stacked = jnp.concatenate([grad_gate, grad_up], axis=1).astype(jnp.bfloat16)
    row_grads = jnp.dot(stacked, weight_in.T, preferred_element_type=jnp.float32).astype(
        jnp.bfloat16
    )
    return (row_grads, prob_grad)


def body(tokens, cotangent, gate_probs, experts, stratum, token_level, w_gate_up, w_down):
    axes = ("node", "local")
    device_count = lax.axis_size(axes)
    token_rows, chosen_count = experts.shape
    width = tokens.shape[1]
    capacity = max(2, token_rows * chosen_count * 5 // (4 * device_count))
    stratum_here = stratum[0]
    masked = token_level * STRATA < (stratum_here + 1) * LEVELS
    loss_weight = jnp.where(
        masked, STRATA / (stratum_here + 1).astype(jnp.float32), jnp.float32(0.0)
    )
    upstream = (cotangent.astype(jnp.float32) * loss_weight[:, None]).astype(jnp.bfloat16)
    chosen = experts.reshape(-1)
    pair_count = chosen.shape[0]
    onehot = (chosen[:, None] == jnp.arange(device_count, dtype=jnp.int32)[None, :]).astype(
        jnp.int32
    )
    ranking = jnp.sum((jnp.cumsum(onehot, axis=0) - 1) * onehot, axis=1)
    placed = chosen * capacity + ranking
    owner_table = jnp.full((device_count * capacity,), pair_count, jnp.int32)
    owner_table = owner_table.at[placed].set(jnp.arange(pair_count, dtype=jnp.int32))
    token_index = (owner_table // chosen_count).reshape(device_count, capacity)
    padded_tokens = jnp.concatenate([tokens, jnp.zeros((1, width), jnp.bfloat16)], axis=0)
    padded_upstream = jnp.concatenate([upstream, jnp.zeros((1, width), jnp.bfloat16)], axis=0)
    weight_in = w_gate_up[0]
    weight_out = w_down[0]
    sizes = CHUNK_SIZES if sum(CHUNK_SIZES) == capacity else (capacity,)
    starts = [sum(sizes[:c]) for c in range(len(sizes))]
    tiled = all((n * width) % (16 * 128) == 0 for n in sizes)
    rows = 16 if tiled else 1

    def block_of(n):
        return (device_count, rows, n * width // rows)

    def exchange(part):
        return lax.all_to_all(part, axes, 0, 0, tiled=True)

    sources = jnp.concatenate([padded_tokens, padded_upstream], axis=0)

    def send_of(c):
        index = token_index[:, starts[c] : starts[c] + sizes[c]]
        index = jnp.stack([index, index + (token_rows + 1)], axis=1).reshape(-1)
        return sources[index].reshape(device_count, 2 * rows, sizes[c] * width // rows)

    def compute(c, arrived):
        n = sizes[c]
        row_grads, prob_grad = expert_grads(
            arrived[:, :rows].reshape(device_count * n, width),
            arrived[:, rows:].reshape(device_count * n, width),
            weight_in,
            weight_out,
        )
        return row_grads.reshape(block_of(n)), prob_grad.reshape(device_count, n)

    def combine(c, home):
        n = sizes[c]
        local = ranking - starts[c]
        inside = (local >= 0) & (local < n)
        slot = jnp.where(inside, chosen * n + local, -1).reshape(token_rows, chosen_count)
        weight = jnp.where(inside.reshape(token_rows, chosen_count), gate_probs, 0.0)
        table = jnp.sum(
            jnp.where(
                slot[:, :, None] == jnp.arange(device_count * n, dtype=jnp.int32)[None, None, :],
                weight[:, :, None],
                0.0,
            ),
            axis=1,
        )
        high = table.astype(jnp.bfloat16)
        low = (table - high.astype(jnp.float32)).astype(jnp.bfloat16)
        home = home.reshape(device_count * n, width)
        return jnp.dot(high, home, preferred_element_type=jnp.float32) + jnp.dot(
            low, home, preferred_element_type=jnp.float32
        )

    last = len(sizes) - 1
    extra = rows * 128 if rows * 128 >= capacity else capacity
    extra_cols = extra // rows

    order = [((), (0,))]
    if last >= 1:
        order.append(((), (1,)))
    for c in range(2, len(sizes)):
        if sizes[c - 2] == sizes[c]:
            order.append(((c - 2,), (c,)))
        else:
            order += [((c - 2,), ()), ((), (c,))]
    for c in range(max(0, len(sizes) - 2), len(sizes)):
        order.append(((c,), ()))

    def final_block():
        probs = jnp.concatenate([prob_parts[i] for i in range(len(sizes))], axis=1)
        probs = jnp.pad(probs, ((0, 0), (0, extra - capacity))).reshape(
            device_count, rows, extra_cols
        )
        return jnp.concatenate([row_grads[last], probs], axis=2)

    arrived = {}
    returned = {}
    row_grads = {}
    prob_parts = {}

    def buffer_of(k):
        backs, sends = order[k]
        parts = [final_block() if n == last else row_grads[n] for n in backs]
        parts += [send_of(n) for n in sends]
        return parts[0] if len(parts) == 1 else jnp.concatenate(parts, axis=1)

    grad_tokens = None
    buffer = buffer_of(0)
    for k, (backs, sends) in enumerate(order):
        done = exchange(buffer)
        computed = [n for n in (order[k + 1][0] if k + 1 < len(order) else ())]
        combined = [n for n in (order[k - 1][0] if k >= 1 else ()) if n < last]
        for n in computed:
            row_grads[n], prob_parts[n] = compute(n, arrived[n])
        for n in combined:
            part = combine(n, returned[n])
            grad_tokens = part if grad_tokens is None else grad_tokens + part
        buffer = buffer_of(k + 1) if k + 1 < len(order) else None
        covered = (buffer, grad_tokens if combined else None)
        done, covered = lax.optimization_barrier((done, covered))
        buffer = covered[0]
        if combined:
            grad_tokens = covered[1]
        offset = 0
        for n in backs:
            returned[n] = done[:, offset : offset + rows] if len(backs) + len(sends) > 1 else done
            offset += rows
        for n in sends:
            arrived[n] = done[:, offset : offset + 2 * rows] if len(backs) + len(sends) > 1 else done
            offset += 2 * rows
    pending = returned[last]
    row_cols = sizes[last] * width // rows
    part = combine(last, pending[:, :, :row_cols])
    grad_tokens = part if grad_tokens is None else grad_tokens + part
    home_probs = pending[:, :, row_cols:].reshape(device_count, extra)[:, :capacity].reshape(-1)
    pick = placed[:, None] == jnp.arange(device_count * capacity, dtype=jnp.int32)[None, :]
    grad_probs = jnp.sum(
        jnp.where(pick, home_probs.astype(jnp.float32)[None, :], 0.0), axis=1
    ).astype(jnp.bfloat16)
    grad_probs = grad_probs.reshape(token_rows, chosen_count)
    return (grad_tokens.astype(jnp.bfloat16), grad_probs)


def solution(mesh):
    placed = (
        P(("node", "local"), None),
        P(("node", "local"), None),
        P(("node", "local"), None),
        P(("node", "local"), None),
        P(("node", "local")),
        P(("node", "local")),
        P(("node", "local"), None, None),
        P(("node", "local"), None, None),
    )
    return jax.shard_map(
        body,
        mesh=mesh,
        in_specs=placed,
        out_specs=(P(("node", "local"), None), P(("node", "local"), None)),
        check_vma=False,
    )
```

profile of v0, /device:TPU:1, one launch (start us, length us, event | category | flops | bytes accessed | tf_op | source)
XLA Modules:
  0.0 497.1 jit_solution(8621937182747177456)
XLA Ops:
  15.6 12.2 %reshape.277 = bf16[128,32,768]{2,1,0:T(8,128)(2,1)} reshape(bf16[768,4096]{1,0:T(8,128)(2,1)} %gather_fusion) | data formatting | bytes 12582912 | tf_op jit(solution)/shard_map/reshape | solution.py:72
  27.8 11.9 %all-to-all-start = ((bf16[128,32,768]{2,1,0:T(8,128)(2,1)}), bf16[128,32,768]{2,1,0:T(8,128)(2,1)}, u32[]{:S(2)}, u32[]{:S(2)}) async-start(bf16[128,32,768]{2,1,0:T(8,128)(2,1)} %reshape.277), calls=%async_computation | async-start | bytes 12582912 | tf_op jit(solution)/shard_map/all_to_all | solution.py:65
  40.1 7.8 %gather_fusion.1 = bf16[1024,4096]{1,0:T(8,128)(2,1)} fusion(bf16[258,4096]{1,0:T(8,128)(2,1)S(1)} %pad_maximum_fusion.2, s32[1024]{0:T(1024)S(1)} %broadcast_clamp_fusion), kind=kCustom, calls=%fused_computation.1 | custom fusion | bytes 16781312 | tf_op jit(solution)/shard_map/gather | solution.py:72
  47.9 13.9 %reshape.279 = bf16[128,32,1024]{2,1,0:T(8,128)(2,1)} reshape(bf16[1024,4096]{1,0:T(8,128)(2,1)} %gather_fusion.1) | data formatting | bytes 16777216 | tf_op jit(solution)/shard_map/reshape | solution.py:72
  61.8 53.2 %all-to-all-done = bf16[128,32,768]{2,1,0:T(8,128)(2,1)} async-done(((bf16[128,32,768]{2,1,0:T(8,128)(2,1)}), bf16[128,32,768]{2,1,0:T(8,128)(2,1)}, u32[]{:S(2)}, u32[]{:S(2)}) %all-to-all-start) | async-done | bytes 6291488 | tf_op jit(solution)/shard_map/all_to_all | solution.py:65
  127.2 12.2 %reshape.284 = bf16[128,32,768]{2,1,0:T(8,128)(2,1)} reshape(bf16[768,4096]{1,0:T(8,128)(2,1)} %gather_fusion.2) | data formatting | bytes 12582912 | tf_op jit(solution)/shard_map/reshape | solution.py:72
  155.8 6.9 %fusion.10 = f32[384,1024]{1,0:T(8,128)S(1)} fusion(bf16[384,4096]{1,0:T(8,128)(2,1)} %reshape.281, bf16[1,4096,1024]{2,1,0:T(8,128)(2,1)} %param.14), kind=kOutput, calls=%fused_computation.15 | convolution fusion | flops 3221225472 | bytes 13107200 | tf_op jit(solution)/shard_map/dot_general | solution.py:13
  164.9 10.4 %fusion.15 = bf16[384,4096]{1,0:T(8,128)(2,1)} fusion(bf16[1,4096,1024]{2,1,0:T(8,128)(2,1)} %param.14, bf16[384,512]{1,0:T(8,128)(2,1)S(1)} %get-tuple-element.44, bf16[384,512]{1,0:T(8,128)(2,1)S(1)} %get-tuple-element.45), kind=kOutput, calls=%fused_computation.18 | convolution fusion | flops 3224371200 | bytes 12320768 | tf_op jit(solution)/shard_map/dot_general | solution.py:24
  181.0 7.0 %pad_maximum_fusion = bf16[128,48,768]{2,1,0:T(8,128)(2,1)} fusion(bf16[128,32,768]{2,1,0:T(8,128)(2,1)} %reshape.284, bf16[128,16,768]{2,1,0:T(8,128)(2,1)S(1)} %reshape.282), kind=kLoop, calls=%fused_computation.4 | loop fusion | flops 18874368 | bytes 18874368 | tf_op jit(solution)/shard_map/concatenate | solution.py:136
  188.1 32.6 %all-to-all-done.1 = bf16[128,32,1024]{2,1,0:T(8,128)(2,1)} async-done(((bf16[128,32,1024]{2,1,0:T(8,128)(2,1)}), bf16[128,32,1024]{2,1,0:T(8,128)(2,1)}, u32[]{:S(2)}, u32[]{:S(2)}) %all-to-all-start.1) | async-done | bytes 8388640 | tf_op jit(solution)/shard_map/all_to_all | solution.py:65
  220.6 10.0 %all-to-all-start.2 = ((bf16[128,48,768]{2,1,0:T(8,128)(2,1)}), bf16[128,48,768]{2,1,0:T(8,128)(2,1)}, u32[]{:S(2)}, u32[]{:S(2)}) async-start(bf16[128,48,768]{2,1,0:T(8,128)(2,1)} %pad_maximum_fusion), calls=%async_computation.2 | async-start | bytes 18874368 | tf_op jit(solution)/shard_map/all_to_all | solution.py:65
  239.0 7.5 %reshape.286 = bf16[512,4096]{1,0:T(8,128)(2,1)} reshape(bf16[128,16,1024]{2,1,0:T(8,128)(2,1)} %get-tuple-element.33) | data formatting | bytes 8388608 | tf_op jit(solution)/shard_map/reshape | solution.py:77
  246.5 7.5 %reshape.285 = bf16[512,4096]{1,0:T(8,128)(2,1)} reshape(bf16[128,16,1024]{2,1,0:T(8,128)(2,1)} %get-tuple-element.34) | data formatting | bytes 8388608 | tf_op jit(solution)/shard_map/reshape | solution.py:78
  254.1 8.4 %fusion.6 = f32[512,1024]{0,1:T(8,128)S(1)} fusion(bf16[512,4096]{1,0:T(8,128)(2,1)} %reshape.286, bf16[1,4096,1024]{2,1,0:T(8,128)(2,1)} %param.14), kind=kOutput, calls=%fused_computation.11 | convolution fusion | flops 4294967296 | bytes 14680064 | tf_op jit(solution)/shard_map/dot_general | solution.py:13
  265.3 9.7 %fusion.12 = bf16[512,4096]{1,0:T(8,128)(2,1)} fusion(bf16[1,4096,1024]{2,1,0:T(8,128)(2,1)} %param.14, bf16[512,512]{0,1:T(8,128)(2,1)S(1)} %get-tuple-element.38, bf16[512,512]{0,1:T(8,128)(2,1)S(1)} %get-tuple-element.39), kind=kOutput, calls=%fused_computation.17 | convolution fusion | flops 4299161600 | bytes 13631488 | tf_op jit(solution)/shard_map/dot_general | solution.py:24
  275.0 7.5 %reshape.287 = bf16[128,16,1024]{2,1,0:T(8,128)(2,1)} reshape(bf16[512,4096]{1,0:T(8,128)(2,1)} %fusion.12) | data formatting | bytes 8388608 | tf_op jit(solution)/shard_map/reshape | solution.py:82
  282.7 62.5 %all-to-all-done.2 = bf16[128,48,768]{2,1,0:T(8,128)(2,1)} async-done(((bf16[128,48,768]{2,1,0:T(8,128)(2,1)}), bf16[128,48,768]{2,1,0:T(8,128)(2,1)}, u32[]{:S(2)}, u32[]{:S(2)}) %all-to-all-start.2) | async-done | bytes 9437216 | tf_op jit(solution)/shard_map/all_to_all | solution.py:65
  345.2 13.2 %all-to-all-start.3 = ((bf16[128,16,1024]{2,1,0:T(8,128)(2,1)}), bf16[128,16,1024]{2,1,0:T(8,128)(2,1)}, u32[]{:S(2)}, u32[]{:S(2)}) async-start(bf16[128,16,1024]{2,1,0:T(8,128)(2,1)} %reshape.287), calls=%async_computation.3 | async-start | bytes 8388608 | tf_op jit(solution)/shard_map/all_to_all | solution.py:65
  358.5 6.8 %fusion.72 = (bf16[128,16,768]{2,1,0:T(8,128)(2,1)}, bf16[128,16,768]{2,1,0:T(8,128)(2,1)}, bf16[128,16,768]{2,1,0:T(8,128)(2,1)}) fusion(bf16[128,48,768]{2,1,0:T(8,128)(2,1)} %all-to-all-done.2), kind=kLoop, calls=%fused_computation.143 | loop fusion | bytes 18874368 | tf_op jit(solution)/shard_map/slice | solution.py:157
  384.4 6.9 %fusion.2 = f32[384,1024]{1,0:T(8,128)S(1)} fusion(bf16[384,4096]{1,0:T(8,128)(2,1)} %reshape.289, bf16[1,4096,1024]{2,1,0:T(8,128)(2,1)} %param.14), kind=kOutput, calls=%fused_computation.7 | convolution fusion | flops 3221225472 | bytes 13107200 | tf_op jit(solution)/shard_map/dot_general | solution.py:13
  393.5 10.4 %fusion.18 = bf16[384,4096]{1,0:T(8,128)(2,1)} fusion(bf16[1,4096,1024]{2,1,0:T(8,128)(2,1)} %param.14, bf16[384,512]{1,0:T(8,128)(2,1)S(1)} %get-tuple-element.42, bf16[384,512]{1,0:T(8,128)(2,1)S(1)} %get-tuple-element.40), kind=kOutput, calls=%fused_computation.19 | convolution fusion | flops 3224371200 | bytes 12320768 | tf_op jit(solution)/shard_map/dot_general | solution.py:24
  422.3 10.1 %all-to-all-start.4 = ((bf16[128,16,896]{2,1,0:T(8,128)(2,1)}), bf16[128,16,896]{2,1,0:T(8,128)(2,1)}, u32[]{:S(2)}, u32[]{:S(2)}) async-start(bf16[128,16,896]{2,1,0:T(8,128)(2,1)} %pad_maximum_fusion.1), calls=%async_computation.4 | async-start | bytes 7340032 | tf_op jit(solution)/shard_map/all_to_all | solution.py:65
  433.7 7.5 %reshape.293 = bf16[512,4096]{1,0:T(8,128)(2,1)} reshape(bf16[128,16,1024]{2,1,0:T(8,128)(2,1)} %all-to-all-done.3) | data formatting | bytes 8388608 | tf_op jit(solution)/shard_map/reshape | solution.py:100
  447.6 31.6 %all-to-all-done.4 = bf16[128,16,896]{2,1,0:T(8,128)(2,1)} async-done(((bf16[128,16,896]{2,1,0:T(8,128)(2,1)}), bf16[128,16,896]{2,1,0:T(8,128)(2,1)}, u32[]{:S(2)}, u32[]{:S(2)}) %all-to-all-start.4) | async-done | bytes 3670048 | tf_op jit(solution)/shard_map/all_to_all | solution.py:65
  (121 shorter events, 126.9 us)
Async XLA Ops:
  0.6 8.6 %copy-start.12 = (s32[128]{0:T(128)S(1)}, s32[128]{0:T(128)}, u32[]{:S(2)}) copy-start(s32[128]{0:T(128)} %param.13) | copy-start | bytes 1540
  0.6 8.6 %copy-start.6 = (bf16[128,4096]{1,0:T(8,128)(2,1)S(1)}, bf16[128,4096]{1,0:T(8,128)(2,1)}, u32[]{:S(2)}) copy-start(bf16[128,4096]{1,0:T(8,128)(2,1)} %param.9) | copy-start | bytes 3145732
  1.7 6.4 %copy-start.9 = (s32[1024]{0:T(1024)}, s32[1024]{0:T(1024)S(1)}, u32[]{:S(2)}) copy-start(s32[1024]{0:T(1024)S(1)} %eq.77) | copy-start | bytes 12292
  2.8 6.7 %copy-start.7 = (bf16[128,4096]{1,0:T(8,128)(2,1)S(1)}, bf16[128,4096]{1,0:T(8,128)(2,1)}, u32[]{:S(2)}) copy-start(bf16[128,4096]{1,0:T(8,128)(2,1)} %param.8) | copy-start | bytes 3145732
  27.8 87.3 %all-to-all-start = ((bf16[128,32,768]{2,1,0:T(8,128)(2,1)}), bf16[128,32,768]{2,1,0:T(8,128)(2,1)}, u32[]{:S(2)}, u32[]{:S(2)}) async-start(bf16[128,32,768]{2,1,0:T(8,128)(2,1)} %reshape.277), calls=%async_computation | async-start | bytes 12582912 | tf_op jit(solution)/shard_map/all_to_all | solution.py:65
  115.1 105.5 %all-to-all-start.1 = ((bf16[128,32,1024]{2,1,0:T(8,128)(2,1)}), bf16[128,32,1024]{2,1,0:T(8,128)(2,1)}, u32[]{:S(2)}, u32[]{:S(2)}) async-start(bf16[128,32,1024]{2,1,0:T(8,128)(2,1)} %reshape.279), calls=%async_computation.1 | async-start | bytes 16777216 | tf_op jit(solution)/shard_map/all_to_all | solution.py:65
  155.8 6.9 %copy-start.4 = (bf16[384,4096]{1,0:T(8,128)(2,1)S(1)}, bf16[384,4096]{1,0:T(8,128)(2,1)}, u32[]{:S(2)}) copy-start(bf16[384,4096]{1,0:T(8,128)(2,1)} %reshape.280) | copy-start | bytes 9437188
  155.8 6.9 %copy-start.13 = (bf16[1,512,4096]{2,1,0:T(8,128)(2,1)S(1)}, bf16[1,512,4096]{2,1,0:T(8,128)(2,1)}, u32[]{:S(2)}) copy-start(bf16[1,512,4096]{2,1,0:T(8,128)(2,1)} %param.15) | copy-start | bytes 12582916
  188.1 42.9 %copy-start.11 = (f32[128,8]{0,1:T(8,128)S(1)}, f32[128,8]{0,1:T(8,128)}, u32[]{:S(2)}) copy-start(f32[128,8]{0,1:T(8,128)} %param.10) | copy-start | bytes 12292
  220.6 124.6 %all-to-all-start.2 = ((bf16[128,48,768]{2,1,0:T(8,128)(2,1)}), bf16[128,48,768]{2,1,0:T(8,128)(2,1)}, u32[]{:S(2)}, u32[]{:S(2)}) async-start(bf16[128,48,768]{2,1,0:T(8,128)(2,1)} %pad_maximum_fusion), calls=%async_computation.2 | async-start | bytes 18874368 | tf_op jit(solution)/shard_map/all_to_all | solution.py:65
  254.0 8.4 %copy-start.3 = (bf16[512,4096]{1,0:T(8,128)(2,1)S(1)}, bf16[512,4096]{1,0:T(8,128)(2,1)}, u32[]{:S(2)}) copy-start(bf16[512,4096]{1,0:T(8,128)(2,1)} %reshape.285) | copy-start | bytes 12582916
  254.1 8.4 %copy-start.14 = (bf16[1,512,4096]{2,1,0:T(8,128)(2,1)S(1)}, bf16[1,512,4096]{2,1,0:T(8,128)(2,1)}, u32[]{:S(2)}) copy-start(bf16[1,512,4096]{2,1,0:T(8,128)(2,1)} %param.15) | copy-start | bytes 12582916
  345.2 77.1 %all-to-all-start.3 = ((bf16[128,16,1024]{2,1,0:T(8,128)(2,1)}), bf16[128,16,1024]{2,1,0:T(8,128)(2,1)}, u32[]{:S(2)}, u32[]{:S(2)}) async-start(bf16[128,16,1024]{2,1,0:T(8,128)(2,1)} %reshape.287), calls=%async_computation.3 | async-start | bytes 8388608 | tf_op jit(solution)/shard_map/all_to_all | solution.py:65
  384.4 6.9 %copy-start.5 = (bf16[384,4096]{1,0:T(8,128)(2,1)S(1)}, bf16[384,4096]{1,0:T(8,128)(2,1)}, u32[]{:S(2)}) copy-start(bf16[384,4096]{1,0:T(8,128)(2,1)} %reshape.288) | copy-start | bytes 9437188
  384.4 6.9 %copy-start.15 = (bf16[1,512,4096]{2,1,0:T(8,128)(2,1)S(1)}, bf16[1,512,4096]{2,1,0:T(8,128)(2,1)}, u32[]{:S(2)}) copy-start(bf16[1,512,4096]{2,1,0:T(8,128)(2,1)} %param.15) | copy-start | bytes 12582916
  422.3 10.7 %copy-start.8 = (s32[128,8]{1,0:T(8,128)S(1)}, s32[128,8]{1,0:T(8,128)}, u32[]{:S(2)}) copy-start(s32[128,8]{1,0:T(8,128)} %get-tuple-element.51) | copy-start | bytes 12292
  422.3 11.4 %copy-start.10 = (s32[1024]{0:T(1024)S(1)}, s32[1024]{0:T(1024)}, u32[]{:S(2)}) copy-start(s32[1024]{0:T(1024)} %copy-done.9) | copy-start | bytes 12292
  422.3 56.8 %all-to-all-start.4 = ((bf16[128,16,896]{2,1,0:T(8,128)(2,1)}), bf16[128,16,896]{2,1,0:T(8,128)(2,1)}, u32[]{:S(2)}, u32[]{:S(2)}) async-start(bf16[128,16,896]{2,1,0:T(8,128)(2,1)} %pad_maximum_fusion.1), calls=%async_computation.4 | async-start | bytes 7340032 | tf_op jit(solution)/shard_map/all_to_all | solution.py:65
  441.3 3.4 copy-start
  441.3 4.1 copy-start.1
  493.3 1.6 copy-start.2
where the time goes:
time: 506 us; the launch traced here: 497 us
  waiting for transfers between devices  180 us (36%)
  local copies, waits for them, and re-layouts  176 us (35%)
  matrix products  70.2 us (14%)
  starting transfers between devices  51.2 us (10%)
  other arithmetic  17.5 us (3%)
    all_to_all x5, waiting for transfers between devices, exchange(): return lax.all_to_all(part, axes, 0, 0, tiled=True)  180 us
    all_to_all x5, starting transfers between devices, exchange(): return lax.all_to_all(part, axes, 0, 0, tiled=True)  51.2 us
    reshape x3, local copies, waits for them, and re-layouts, send_of(): sources[index].reshape(device_count, 2 * rows, sizes[c] * width // rows)  38.3 us
    dot_general x3, matrix products, expert_grads(): jnp.dot(stacked, weight_in.T, preferred_element_type=jnp.float32)  30.4 us
    dot_general x3, matrix products, expert_grads(): projected = jnp.dot(inputs, weight_in, preferred_element_type=jnp.float32)  22.2 us
    reshape x3, local copies, waits for them, and re-layouts, compute(): arrived[:, :rows].reshape(device_count * n, width)  21.1 us
    reshape x3, local copies, waits for them, and re-layouts, compute(): return (row_grads.reshape(block_of(n)), prob_grad.reshape(device_count, n))  20 us
    gather x3, local copies, waits for them, and re-layouts, send_of(): sources[index].reshape(device_count, 2 * rows, sizes[c] * width // rows)  19.3 us
  transfers between devices with their start and end apart: 5, of which 4 were waited for; matrix products, arithmetic and copies ran while one was open for 44% of the time, Pallas kernels for 0%

commit v1 on v0

--- a/solution.py
+++ b/solution.py
@@ -136,11 +136,15 @@
         return parts[0] if len(parts) == 1 else jnp.concatenate(parts, axis=1)
 
     grad_tokens = None
+    summed = set()
     buffer = buffer_of(0)
     for k, (backs, sends) in enumerate(order):
         done = exchange(buffer)
         computed = [n for n in (order[k + 1][0] if k + 1 < len(order) else ())]
-        combined = [n for n in (order[k - 1][0] if k >= 1 else ()) if n < last]
+        combined = []
+        if not computed:
+            combined = [n for n in sorted(returned) if n < last and n not in summed]
+            summed.update(combined)
         for n in computed:
             row_grads[n], prob_parts[n] = compute(n, arrived[n])
         for n in combined:

time: 506 us -> 492 us (0.972)
  waiting for transfers between devices: 180 us -> 173 us
  local copies, waits for them, and re-layouts: 176 us -> 170 us
    all_to_all x5, waiting for transfers between devices: 180 us -> 173 us  [exchange(): return lax.all_to_all(part, axes, 0, 0, tiled=True)]
  transfers between devices with their start and end apart: 5 -> 5, of which waited for: 4 -> 5; matrix products, arithmetic and copies ran while one was open for 44% -> 44% of each run, Pallas kernels for 0% -> 0%
where the time goes in v1:
time: 492 us; the launch traced here: 484 us
  waiting for transfers between devices  173 us (35%)
  local copies, waits for them, and re-layouts  170 us (35%)
  matrix products  71 us (14%)
  starting transfers between devices  49.1 us (10%)
  other arithmetic  18 us (4%)
    all_to_all x5, waiting for transfers between devices, exchange(): return lax.all_to_all(part, axes, 0, 0, tiled=True)  173 us
    all_to_all x5, starting transfers between devices, exchange(): return lax.all_to_all(part, axes, 0, 0, tiled=True)  49.1 us
    reshape x3, local copies, waits for them, and re-layouts, send_of(): sources[index].reshape(device_count, 2 * rows, sizes[c] * width // rows)  38.3 us
    dot_general x3, matrix products, expert_grads(): jnp.dot(stacked, weight_in.T, preferred_element_type=jnp.float32)  30.3 us
    dot_general x3, matrix products, expert_grads(): projected = jnp.dot(inputs, weight_in, preferred_element_type=jnp.float32)  22.2 us
    reshape x3, local copies, waits for them, and re-layouts, compute(): arrived[:, :rows].reshape(device_count * n, width)  21 us
    gather x3, local copies, waits for them, and re-layouts, send_of(): sources[index].reshape(device_count, 2 * rows, sizes[c] * width // rows)  19.2 us
    reshape x3, local copies, waits for them, and re-layouts, compute(): return (row_grads.reshape(block_of(n)), prob_grad.reshape(device_count, n))  18.9 us
  transfers between devices with their start and end apart: 5, of which 5 were waited for; matrix products, arithmetic and copies ran while one was open for 44% of the time, Pallas kernels for 0%

profile of v1, /device:TPU:1, one launch (start us, length us, event | category | flops | bytes accessed | tf_op | source)
XLA Modules:
  0.0 483.7 jit_solution(15015569173503429274)
XLA Ops:
  16.2 12.2 %reshape.277 = bf16[128,32,768]{2,1,0:T(8,128)(2,1)} reshape(bf16[768,4096]{1,0:T(8,128)(2,1)} %gather_fusion) | data formatting | bytes 12582912 | tf_op jit(solution)/shard_map/reshape | solution.py:72
  28.4 11.9 %all-to-all-start = ((bf16[128,32,768]{2,1,0:T(8,128)(2,1)}), bf16[128,32,768]{2,1,0:T(8,128)(2,1)}, u32[]{:S(2)}, u32[]{:S(2)}) async-start(bf16[128,32,768]{2,1,0:T(8,128)(2,1)} %reshape.277), calls=%async_computation | async-start | bytes 12582912 | tf_op jit(solution)/shard_map/all_to_all | solution.py:65
  40.7 7.8 %gather_fusion.1 = bf16[1024,4096]{1,0:T(8,128)(2,1)} fusion(bf16[258,4096]{1,0:T(8,128)(2,1)S(1)} %pad_maximum_fusion.2, s32[1024]{0:T(1024)S(1)} %broadcast_clamp_fusion), kind=kCustom, calls=%fused_computation.1 | custom fusion | bytes 16781312 | tf_op jit(solution)/shard_map/gather | solution.py:72
  48.5 14.0 %reshape.279 = bf16[128,32,1024]{2,1,0:T(8,128)(2,1)} reshape(bf16[1024,4096]{1,0:T(8,128)(2,1)} %gather_fusion.1) | data formatting | bytes 16777216 | tf_op jit(solution)/shard_map/reshape | solution.py:72
  62.5 53.2 %all-to-all-done = bf16[128,32,768]{2,1,0:T(8,128)(2,1)} async-done(((bf16[128,32,768]{2,1,0:T(8,128)(2,1)}), bf16[128,32,768]{2,1,0:T(8,128)(2,1)}, u32[]{:S(2)}, u32[]{:S(2)}) %all-to-all-start) | async-done | bytes 6291488 | tf_op jit(solution)/shard_map/all_to_all | solution.py:65
  127.8 12.2 %reshape.284 = bf16[128,32,768]{2,1,0:T(8,128)(2,1)} reshape(bf16[768,4096]{1,0:T(8,128)(2,1)} %gather_fusion.2) | data formatting | bytes 12582912 | tf_op jit(solution)/shard_map/reshape | solution.py:72
  145.0 6.7 %reshape.281 = bf16[384,4096]{1,0:T(8,128)(2,1)} reshape(bf16[128,16,768]{2,1,0:T(8,128)(2,1)} %get-tuple-element.33) | data formatting | bytes 6291456 | tf_op jit(solution)/shard_map/reshape | solution.py:77
  156.3 6.9 %fusion.10 = f32[384,1024]{1,0:T(8,128)S(1)} fusion(bf16[384,4096]{1,0:T(8,128)(2,1)} %reshape.281, bf16[1,4096,1024]{2,1,0:T(8,128)(2,1)} %param.14), kind=kOutput, calls=%fused_computation.15 | convolution fusion | flops 3221225472 | bytes 13107200 | tf_op jit(solution)/shard_map/dot_general | solution.py:13
  165.4 10.3 %fusion.15 = bf16[384,4096]{1,0:T(8,128)(2,1)} fusion(bf16[1,4096,1024]{2,1,0:T(8,128)(2,1)} %param.14, bf16[384,512]{1,0:T(8,128)(2,1)S(1)} %get-tuple-element.42, bf16[384,512]{1,0:T(8,128)(2,1)S(1)} %get-tuple-element.43), kind=kOutput, calls=%fused_computation.18 | convolution fusion | flops 3224371200 | bytes 12320768 | tf_op jit(solution)/shard_map/dot_general | solution.py:24
  181.5 7.0 %pad_maximum_fusion = bf16[128,48,768]{2,1,0:T(8,128)(2,1)} fusion(bf16[128,32,768]{2,1,0:T(8,128)(2,1)} %reshape.284, bf16[128,16,768]{2,1,0:T(8,128)(2,1)S(1)} %reshape.282), kind=kLoop, calls=%fused_computation.4 | loop fusion | flops 18874368 | bytes 18874368 | tf_op jit(solution)/shard_map/concatenate | solution.py:136
  188.5 32.7 %all-to-all-done.1 = bf16[128,32,1024]{2,1,0:T(8,128)(2,1)} async-done(((bf16[128,32,1024]{2,1,0:T(8,128)(2,1)}), bf16[128,32,1024]{2,1,0:T(8,128)(2,1)}, u32[]{:S(2)}, u32[]{:S(2)}) %all-to-all-start.1) | async-done | bytes 8388640 | tf_op jit(solution)/shard_map/all_to_all | solution.py:65
  221.2 10.0 %all-to-all-start.2 = ((bf16[128,48,768]{2,1,0:T(8,128)(2,1)}), bf16[128,48,768]{2,1,0:T(8,128)(2,1)}, u32[]{:S(2)}, u32[]{:S(2)}) async-start(bf16[128,48,768]{2,1,0:T(8,128)(2,1)} %pad_maximum_fusion), calls=%async_computation.2 | async-start | bytes 18874368 | tf_op jit(solution)/shard_map/all_to_all | solution.py:65
  237.6 7.5 %reshape.286 = bf16[512,4096]{1,0:T(8,128)(2,1)} reshape(bf16[128,16,1024]{2,1,0:T(8,128)(2,1)} %get-tuple-element.31) | data formatting | bytes 8388608 | tf_op jit(solution)/shard_map/reshape | solution.py:77
  245.2 7.6 %reshape.285 = bf16[512,4096]{1,0:T(8,128)(2,1)} reshape(bf16[128,16,1024]{2,1,0:T(8,128)(2,1)} %get-tuple-element.32) | data formatting | bytes 8388608 | tf_op jit(solution)/shard_map/reshape | solution.py:78
  252.7 8.4 %fusion.6 = f32[512,1024]{0,1:T(8,128)S(1)} fusion(bf16[512,4096]{1,0:T(8,128)(2,1)} %reshape.286, bf16[1,4096,1024]{2,1,0:T(8,128)(2,1)} %param.14), kind=kOutput, calls=%fused_computation.11 | convolution fusion | flops 4294967296 | bytes 14680064 | tf_op jit(solution)/shard_map/dot_general | solution.py:13
  263.9 9.6 %fusion.12 = bf16[512,4096]{1,0:T(8,128)(2,1)} fusion(bf16[1,4096,1024]{2,1,0:T(8,128)(2,1)} %param.14, bf16[512,512]{0,1:T(8,128)(2,1)S(1)} %get-tuple-element.36, bf16[512,512]{0,1:T(8,128)(2,1)S(1)} %get-tuple-element.37), kind=kOutput, calls=%fused_computation.17 | convolution fusion | flops 4299161600 | bytes 13631488 | tf_op jit(solution)/shard_map/dot_general | solution.py:24
  273.6 7.6 %reshape.287 = bf16[128,16,1024]{2,1,0:T(8,128)(2,1)} reshape(bf16[512,4096]{1,0:T(8,128)(2,1)} %fusion.12) | data formatting | bytes 8388608 | tf_op jit(solution)/shard_map/reshape | solution.py:82
  281.1 64.7 %all-to-all-done.2 = bf16[128,48,768]{2,1,0:T(8,128)(2,1)} async-done(((bf16[128,48,768]{2,1,0:T(8,128)(2,1)}), bf16[128,48,768]{2,1,0:T(8,128)(2,1)}, u32[]{:S(2)}, u32[]{:S(2)}) %all-to-all-start.2) | async-done | bytes 9437216 | tf_op jit(solution)/shard_map/all_to_all | solution.py:65
  345.9 13.2 %all-to-all-start.3 = ((bf16[128,16,1024]{2,1,0:T(8,128)(2,1)}), bf16[128,16,1024]{2,1,0:T(8,128)(2,1)}, u32[]{:S(2)}, u32[]{:S(2)}) async-start(bf16[128,16,1024]{2,1,0:T(8,128)(2,1)} %reshape.287), calls=%async_computation.3 | async-start | bytes 8388608 | tf_op jit(solution)/shard_map/all_to_all | solution.py:65
  376.9 6.9 %fusion.2 = f32[384,1024]{1,0:T(8,128)S(1)} fusion(bf16[384,4096]{1,0:T(8,128)(2,1)} %reshape.289, bf16[1,4096,1024]{2,1,0:T(8,128)(2,1)} %param.14), kind=kOutput, calls=%fused_computation.7 | convolution fusion | flops 3221225472 | bytes 13107200 | tf_op jit(solution)/shard_map/dot_general | solution.py:13
  386.0 10.3 %fusion.18 = bf16[384,4096]{1,0:T(8,128)(2,1)} fusion(bf16[1,4096,1024]{2,1,0:T(8,128)(2,1)} %param.14, bf16[384,512]{1,0:T(8,128)(2,1)S(1)} %get-tuple-element.40, bf16[384,512]{1,0:T(8,128)(2,1)S(1)} %get-tuple-element.38), kind=kOutput, calls=%fused_computation.19 | convolution fusion | flops 3224371200 | bytes 12320768 | tf_op jit(solution)/shard_map/dot_general | solution.py:24
  411.2 8.0 %all-to-all-start.4 = ((bf16[128,16,896]{2,1,0:T(8,128)(2,1)}), bf16[128,16,896]{2,1,0:T(8,128)(2,1)}, u32[]{:S(2)}, u32[]{:S(2)}) async-start(bf16[128,16,896]{2,1,0:T(8,128)(2,1)} %pad_maximum_fusion.1), calls=%async_computation.4 | async-start | bytes 7340032 | tf_op jit(solution)/shard_map/all_to_all | solution.py:65
  432.3 7.5 %reshape.293 = bf16[512,4096]{1,0:T(8,128)(2,1)} reshape(bf16[128,16,1024]{2,1,0:T(8,128)(2,1)} %all-to-all-done.3) | data formatting | bytes 8388608 | tf_op jit(solution)/shard_map/reshape | solution.py:100
  446.1 19.6 %all-to-all-done.4 = bf16[128,16,896]{2,1,0:T(8,128)(2,1)} async-done(((bf16[128,16,896]{2,1,0:T(8,128)(2,1)}), bf16[128,16,896]{2,1,0:T(8,128)(2,1)}, u32[]{:S(2)}, u32[]{:S(2)}) %all-to-all-start.4) | async-done | bytes 3670048 | tf_op jit(solution)/shard_map/all_to_all | solution.py:65
  (131 shorter events, 125.4 us)
Async XLA Ops:
  0.6 9.2 %copy-start.17 = (s32[128]{0:T(128)S(1)}, s32[128]{0:T(128)}, u32[]{:S(2)}) copy-start(s32[128]{0:T(128)} %param.13) | copy-start | bytes 1540
  0.6 9.2 %copy-start.8 = (bf16[128,4096]{1,0:T(8,128)(2,1)S(1)}, bf16[128,4096]{1,0:T(8,128)(2,1)}, u32[]{:S(2)}) copy-start(bf16[128,4096]{1,0:T(8,128)(2,1)} %param.9) | copy-start | bytes 3145732
  1.7 8.4 %copy-start.12 = (s32[1024]{0:T(1024)}, s32[1024]{0:T(1024)S(1)}, u32[]{:S(2)}) copy-start(s32[1024]{0:T(1024)S(1)} %eq.77) | copy-start | bytes 12292
  3.4 6.8 %copy-start.9 = (bf16[128,4096]{1,0:T(8,128)(2,1)S(1)}, bf16[128,4096]{1,0:T(8,128)(2,1)}, u32[]{:S(2)}) copy-start(bf16[128,4096]{1,0:T(8,128)(2,1)} %param.8) | copy-start | bytes 3145732
  4.1 6.0 %copy-start.10 = (s32[1024]{0:T(1024)}, s32[1024]{0:T(1024)S(1)}, u32[]{:S(2)}) copy-start(s32[1024]{0:T(1024)S(1)} %fusion.47) | copy-start | bytes 12292
  28.4 87.3 %all-to-all-start = ((bf16[128,32,768]{2,1,0:T(8,128)(2,1)}), bf16[128,32,768]{2,1,0:T(8,128)(2,1)}, u32[]{:S(2)}, u32[]{:S(2)}) async-start(bf16[128,32,768]{2,1,0:T(8,128)(2,1)} %reshape.277), calls=%async_computation | async-start | bytes 12582912 | tf_op jit(solution)/shard_map/all_to_all | solution.py:65
  115.7 105.5 %all-to-all-start.1 = ((bf16[128,32,1024]{2,1,0:T(8,128)(2,1)}), bf16[128,32,1024]{2,1,0:T(8,128)(2,1)}, u32[]{:S(2)}, u32[]{:S(2)}) async-start(bf16[128,32,1024]{2,1,0:T(8,128)(2,1)} %reshape.279), calls=%async_computation.1 | async-start | bytes 16777216 | tf_op jit(solution)/shard_map/all_to_all | solution.py:65
  156.3 6.9 %copy-start.4 = (bf16[384,4096]{1,0:T(8,128)(2,1)S(1)}, bf16[384,4096]{1,0:T(8,128)(2,1)}, u32[]{:S(2)}) copy-start(bf16[384,4096]{1,0:T(8,128)(2,1)} %reshape.280) | copy-start | bytes 9437188
  156.3 6.9 %copy-start.18 = (bf16[1,512,4096]{2,1,0:T(8,128)(2,1)S(1)}, bf16[1,512,4096]{2,1,0:T(8,128)(2,1)}, u32[]{:S(2)}) copy-start(bf16[1,512,4096]{2,1,0:T(8,128)(2,1)} %param.15) | copy-start | bytes 12582916
  221.2 124.6 %all-to-all-start.2 = ((bf16[128,48,768]{2,1,0:T(8,128)(2,1)}), bf16[128,48,768]{2,1,0:T(8,128)(2,1)}, u32[]{:S(2)}, u32[]{:S(2)}) async-start(bf16[128,48,768]{2,1,0:T(8,128)(2,1)} %pad_maximum_fusion), calls=%async_computation.2 | async-start | bytes 18874368 | tf_op jit(solution)/shard_map/all_to_all | solution.py:65
  252.7 8.4 %copy-start.3 = (bf16[512,4096]{1,0:T(8,128)(2,1)S(1)}, bf16[512,4096]{1,0:T(8,128)(2,1)}, u32[]{:S(2)}) copy-start(bf16[512,4096]{1,0:T(8,128)(2,1)} %reshape.285) | copy-start | bytes 12582916
  252.7 8.4 %copy-start.19 = (bf16[1,512,4096]{2,1,0:T(8,128)(2,1)S(1)}, bf16[1,512,4096]{2,1,0:T(8,128)(2,1)}, u32[]{:S(2)}) copy-start(bf16[1,512,4096]{2,1,0:T(8,128)(2,1)} %param.15) | copy-start | bytes 12582916
  345.9 65.4 %all-to-all-start.3 = ((bf16[128,16,1024]{2,1,0:T(8,128)(2,1)}), bf16[128,16,1024]{2,1,0:T(8,128)(2,1)}, u32[]{:S(2)}, u32[]{:S(2)}) async-start(bf16[128,16,1024]{2,1,0:T(8,128)(2,1)} %reshape.287), calls=%async_computation.3 | async-start | bytes 8388608 | tf_op jit(solution)/shard_map/all_to_all | solution.py:65
  376.9 6.9 %copy-start.5 = (bf16[384,4096]{1,0:T(8,128)(2,1)S(1)}, bf16[384,4096]{1,0:T(8,128)(2,1)}, u32[]{:S(2)}) copy-start(bf16[384,4096]{1,0:T(8,128)(2,1)} %reshape.288) | copy-start | bytes 9437188
  376.9 6.9 %copy-start.20 = (bf16[1,512,4096]{2,1,0:T(8,128)(2,1)S(1)}, bf16[1,512,4096]{2,1,0:T(8,128)(2,1)}, u32[]{:S(2)}) copy-start(bf16[1,512,4096]{2,1,0:T(8,128)(2,1)} %param.15) | copy-start | bytes 12582916
  408.6 10.7 %copy-start.11 = (s32[1024]{0:T(1024)S(1)}, s32[1024]{0:T(1024)}, u32[]{:S(2)}) copy-start(s32[1024]{0:T(1024)} %copy-done.10) | copy-start | bytes 12292
  408.6 10.8 %copy-start.15 = (s32[128,8]{0,1:T(8,128)S(1)}, s32[128,8]{0,1:T(8,128)}, u32[]{:S(2)}) copy-start(s32[128,8]{0,1:T(8,128)} %get-tuple-element.58) | copy-start | bytes 12292
  408.6 10.9 %copy-start.14 = (s32[128,8]{0,1:T(8,128)S(1)}, s32[128,8]{0,1:T(8,128)}, u32[]{:S(2)}) copy-start(s32[128,8]{0,1:T(8,128)} %get-tuple-element.56) | copy-start | bytes 12292
  408.6 11.0 %copy-start.16 = (f32[128,8]{0,1:T(8,128)S(1)}, f32[128,8]{0,1:T(8,128)}, u32[]{:S(2)}) copy-start(f32[128,8]{0,1:T(8,128)} %param.10) | copy-start | bytes 12292
  408.6 14.3 %copy-start.13 = (s32[1024]{0:T(1024)S(1)}, s32[1024]{0:T(1024)}, u32[]{:S(2)}) copy-start(s32[1024]{0:T(1024)} %copy-done.12) | copy-start | bytes 12292
  411.2 54.5 %all-to-all-start.4 = ((bf16[128,16,896]{2,1,0:T(8,128)(2,1)}), bf16[128,16,896]{2,1,0:T(8,128)(2,1)}, u32[]{:S(2)}, u32[]{:S(2)}) async-start(bf16[128,16,896]{2,1,0:T(8,128)(2,1)} %pad_maximum_fusion.1), calls=%async_computation.4 | async-start | bytes 7340032 | tf_op jit(solution)/shard_map/all_to_all | solution.py:65
  439.9 3.4 copy-start
  439.9 4.1 copy-start.1
  471.3 8.6 %copy-start.6 = (f32[128,384]{1,0:T(8,128)S(1)}, f32[128,384]{1,0:T(8,128)}, u32[]{:S(2)}) copy-start(f32[128,384]{1,0:T(8,128)} %select_reduce_fusion.2) | copy-start | bytes 589828
  (2 other events, 3.3 us)

commit v2 on v1

--- a/solution.py
+++ b/solution.py
@@ -46,9 +46,11 @@
     )
     ranking = jnp.sum((jnp.cumsum(onehot, axis=0) - 1) * onehot, axis=1)
     placed = chosen * capacity + ranking
-    owner_table = jnp.full((device_count * capacity,), pair_count, jnp.int32)
-    owner_table = owner_table.at[placed].set(jnp.arange(pair_count, dtype=jnp.int32))
-    token_index = (owner_table // chosen_count).reshape(device_count, capacity)
+    holder = placed[None, :] == jnp.arange(device_count * capacity, dtype=jnp.int32)[:, None]
+    token_index = jnp.min(
+        jnp.where(holder, jnp.arange(pair_count, dtype=jnp.int32)[None, :] // chosen_count, token_rows),
+        axis=1,
+    ).reshape(device_count, capacity)
     padded_tokens = jnp.concatenate([tokens, jnp.zeros((1, width), jnp.bfloat16)], axis=0)
     padded_upstream = jnp.concatenate([upstream, jnp.zeros((1, width), jnp.bfloat16)], axis=0)
     weight_in = w_gate_up[0]

time: 492 us -> 488 us (level)
  transfers between devices with their start and end apart: 5 -> 5, of which waited for: 5 -> 5; matrix products, arithmetic and copies ran while one was open for 44% -> 45% of each run, Pallas kernels for 0% -> 0%
where the time goes in v2:
time: 488 us; the launch traced here: 479 us
  waiting for transfers between devices  173 us (35%)
  local copies, waits for them, and re-layouts  166 us (34%)
  matrix products  71.2 us (15%)
  starting transfers between devices  49 us (10%)
  other arithmetic  17.4 us (4%)
    all_to_all x5, waiting for transfers between devices, exchange(): return lax.all_to_all(part, axes, 0, 0, tiled=True)  173 us
    all_to_all x5, starting transfers between devices, exchange(): return lax.all_to_all(part, axes, 0, 0, tiled=True)  49 us
    reshape x3, local copies, waits for them, and re-layouts, send_of(): sources[index].reshape(device_count, 2 * rows, sizes[c] * width // rows)  38.3 us
    dot_general x3, matrix products, expert_grads(): jnp.dot(stacked, weight_in.T, preferred_element_type=jnp.float32)  30.4 us
    dot_general x3, matrix products, expert_grads(): projected = jnp.dot(inputs, weight_in, preferred_element_type=jnp.float32)  22.2 us
    reshape x3, local copies, waits for them, and re-layouts, compute(): arrived[:, :rows].reshape(device_count * n, width)  21 us
    gather x3, local copies, waits for them, and re-layouts, send_of(): sources[index].reshape(device_count, 2 * rows, sizes[c] * width // rows)  19.2 us
    reshape x3, local copies, waits for them, and re-layouts, compute(): return (row_grads.reshape(block_of(n)), prob_grad.reshape(device_count, n))  18.8 us
  transfers between devices with their start and end apart: 5, of which 5 were waited for; matrix products, arithmetic and copies ran while one was open for 45% of the time, Pallas kernels for 0%

profile of v2, /device:TPU:1, one launch (start us, length us, event | category | flops | bytes accessed | tf_op | source)
XLA Modules:
  0.0 479.0 jit_solution(14175236186338290377)
XLA Ops:
  11.6 12.2 %reshape.300 = bf16[128,32,768]{2,1,0:T(8,128)(2,1)} reshape(bf16[768,4096]{1,0:T(8,128)(2,1)} %gather_fusion) | data formatting | bytes 12582912 | tf_op jit(solution)/shard_map/reshape | solution.py:74
  23.8 11.9 %all-to-all-start = ((bf16[128,32,768]{2,1,0:T(8,128)(2,1)}), bf16[128,32,768]{2,1,0:T(8,128)(2,1)}, u32[]{:S(2)}, u32[]{:S(2)}) async-start(bf16[128,32,768]{2,1,0:T(8,128)(2,1)} %reshape.300), calls=%async_computation | async-start | bytes 12582912 | tf_op jit(solution)/shard_map/all_to_all | solution.py:67
  36.2 7.8 %gather_fusion.1 = bf16[1024,4096]{1,0:T(8,128)(2,1)} fusion(bf16[258,4096]{1,0:T(8,128)(2,1)S(1)} %pad_maximum_fusion.2, s32[1024]{0:T(1024)S(1)} %broadcast_clamp_fusion), kind=kCustom, calls=%fused_computation.1 | custom fusion | bytes 16781312 | tf_op jit(solution)/shard_map/gather | solution.py:74
  43.9 13.9 %reshape.302 = bf16[128,32,1024]{2,1,0:T(8,128)(2,1)} reshape(bf16[1024,4096]{1,0:T(8,128)(2,1)} %gather_fusion.1) | data formatting | bytes 16777216 | tf_op jit(solution)/shard_map/reshape | solution.py:74
  57.9 53.2 %all-to-all-done = bf16[128,32,768]{2,1,0:T(8,128)(2,1)} async-done(((bf16[128,32,768]{2,1,0:T(8,128)(2,1)}), bf16[128,32,768]{2,1,0:T(8,128)(2,1)}, u32[]{:S(2)}, u32[]{:S(2)}) %all-to-all-start) | async-done | bytes 6291488 | tf_op jit(solution)/shard_map/all_to_all | solution.py:67
  123.2 12.2 %reshape.307 = bf16[128,32,768]{2,1,0:T(8,128)(2,1)} reshape(bf16[768,4096]{1,0:T(8,128)(2,1)} %gather_fusion.2) | data formatting | bytes 12582912 | tf_op jit(solution)/shard_map/reshape | solution.py:74
  151.7 6.9 %fusion.10 = f32[384,1024]{1,0:T(8,128)S(1)} fusion(bf16[384,4096]{1,0:T(8,128)(2,1)} %reshape.304, bf16[1,4096,1024]{2,1,0:T(8,128)(2,1)} %param.14), kind=kOutput, calls=%fused_computation.14 | convolution fusion | flops 3221225472 | bytes 13107200 | tf_op jit(solution)/shard_map/dot_general | solution.py:13
  160.8 10.3 %fusion.15 = bf16[384,4096]{1,0:T(8,128)(2,1)} fusion(bf16[1,4096,1024]{2,1,0:T(8,128)(2,1)} %param.14, bf16[384,512]{1,0:T(8,128)(2,1)S(1)} %get-tuple-element.42, bf16[384,512]{1,0:T(8,128)(2,1)S(1)} %get-tuple-element.43), kind=kOutput, calls=%fused_computation.17 | convolution fusion | flops 3224371200 | bytes 12320768 | tf_op jit(solution)/shard_map/dot_general | solution.py:24
  176.9 7.0 %pad_maximum_fusion = bf16[128,48,768]{2,1,0:T(8,128)(2,1)} fusion(bf16[128,32,768]{2,1,0:T(8,128)(2,1)} %reshape.307, bf16[128,16,768]{2,1,0:T(8,128)(2,1)S(1)} %reshape.305), kind=kLoop, calls=%fused_computation.3 | loop fusion | flops 18874368 | bytes 18874368 | tf_op jit(solution)/shard_map/concatenate | solution.py:138
  184.0 32.7 %all-to-all-done.1 = bf16[128,32,1024]{2,1,0:T(8,128)(2,1)} async-done(((bf16[128,32,1024]{2,1,0:T(8,128)(2,1)}), bf16[128,32,1024]{2,1,0:T(8,128)(2,1)}, u32[]{:S(2)}, u32[]{:S(2)}) %all-to-all-start.1) | async-done | bytes 8388640 | tf_op jit(solution)/shard_map/all_to_all | solution.py:67
  216.7 10.0 %all-to-all-start.2 = ((bf16[128,48,768]{2,1,0:T(8,128)(2,1)}), bf16[128,48,768]{2,1,0:T(8,128)(2,1)}, u32[]{:S(2)}, u32[]{:S(2)}) async-start(bf16[128,48,768]{2,1,0:T(8,128)(2,1)} %pad_maximum_fusion), calls=%async_computation.2 | async-start | bytes 18874368 | tf_op jit(solution)/shard_map/all_to_all | solution.py:67
  233.0 7.5 %reshape.309 = bf16[512,4096]{1,0:T(8,128)(2,1)} reshape(bf16[128,16,1024]{2,1,0:T(8,128)(2,1)} %get-tuple-element.31) | data formatting | bytes 8388608 | tf_op jit(solution)/shard_map/reshape | solution.py:79
  240.5 7.5 %reshape.308 = bf16[512,4096]{1,0:T(8,128)(2,1)} reshape(bf16[128,16,1024]{2,1,0:T(8,128)(2,1)} %get-tuple-element.32) | data formatting | bytes 8388608 | tf_op jit(solution)/shard_map/reshape | solution.py:80
  248.1 8.4 %fusion.6 = f32[512,1024]{0,1:T(8,128)S(1)} fusion(bf16[512,4096]{1,0:T(8,128)(2,1)} %reshape.309, bf16[1,4096,1024]{2,1,0:T(8,128)(2,1)} %param.14), kind=kOutput, calls=%fused_computation.10 | convolution fusion | flops 4294967296 | bytes 14680064 | tf_op jit(solution)/shard_map/dot_general | solution.py:13
  259.3 9.7 %fusion.12 = bf16[512,4096]{1,0:T(8,128)(2,1)} fusion(bf16[1,4096,1024]{2,1,0:T(8,128)(2,1)} %param.14, bf16[512,512]{0,1:T(8,128)(2,1)S(1)} %get-tuple-element.36, bf16[512,512]{0,1:T(8,128)(2,1)S(1)} %get-tuple-element.37), kind=kOutput, calls=%fused_computation.16 | convolution fusion | flops 4299161600 | bytes 13631488 | tf_op jit(solution)/shard_map/dot_general | solution.py:24
  269.0 7.5 %reshape.310 = bf16[128,16,1024]{2,1,0:T(8,128)(2,1)} reshape(bf16[512,4096]{1,0:T(8,128)(2,1)} %fusion.12) | data formatting | bytes 8388608 | tf_op jit(solution)/shard_map/reshape | solution.py:84
  276.5 64.8 %all-to-all-done.2 = bf16[128,48,768]{2,1,0:T(8,128)(2,1)} async-done(((bf16[128,48,768]{2,1,0:T(8,128)(2,1)}), bf16[128,48,768]{2,1,0:T(8,128)(2,1)}, u32[]{:S(2)}, u32[]{:S(2)}) %all-to-all-start.2) | async-done | bytes 9437216 | tf_op jit(solution)/shard_map/all_to_all | solution.py:67
  341.3 13.2 %all-to-all-start.3 = ((bf16[128,16,1024]{2,1,0:T(8,128)(2,1)}), bf16[128,16,1024]{2,1,0:T(8,128)(2,1)}, u32[]{:S(2)}, u32[]{:S(2)}) async-start(bf16[128,16,1024]{2,1,0:T(8,128)(2,1)} %reshape.310), calls=%async_computation.3 | async-start | bytes 8388608 | tf_op jit(solution)/shard_map/all_to_all | solution.py:67
  361.0 6.7 %reshape.312 = bf16[384,4096]{1,0:T(8,128)(2,1)} reshape(bf16[128,16,768]{2,1,0:T(8,128)(2,1)} %get-tuple-element.29) | data formatting | bytes 6291456 | tf_op jit(solution)/shard_map/reshape | solution.py:79
  372.3 6.9 %fusion.2 = f32[384,1024]{1,0:T(8,128)S(1)} fusion(bf16[384,4096]{1,0:T(8,128)(2,1)} %reshape.312, bf16[1,4096,1024]{2,1,0:T(8,128)(2,1)} %param.14), kind=kOutput, calls=%fused_computation.6 | convolution fusion | flops 3221225472 | bytes 13107200 | tf_op jit(solution)/shard_map/dot_general | solution.py:13
  381.5 10.3 %fusion.18 = bf16[384,4096]{1,0:T(8,128)(2,1)} fusion(bf16[1,4096,1024]{2,1,0:T(8,128)(2,1)} %param.14, bf16[384,512]{1,0:T(8,128)(2,1)S(1)} %get-tuple-element.40, bf16[384,512]{1,0:T(8,128)(2,1)S(1)} %get-tuple-element.38), kind=kOutput, calls=%fused_computation.18 | convolution fusion | flops 3224371200 | bytes 12320768 | tf_op jit(solution)/shard_map/dot_general | solution.py:24
  406.6 8.0 %all-to-all-start.4 = ((bf16[128,16,896]{2,1,0:T(8,128)(2,1)}), bf16[128,16,896]{2,1,0:T(8,128)(2,1)}, u32[]{:S(2)}, u32[]{:S(2)}) async-start(bf16[128,16,896]{2,1,0:T(8,128)(2,1)} %pad_maximum_fusion.1), calls=%async_computation.4 | async-start | bytes 7340032 | tf_op jit(solution)/shard_map/all_to_all | solution.py:67
  427.7 7.5 %reshape.316 = bf16[512,4096]{1,0:T(8,128)(2,1)} reshape(bf16[128,16,1024]{2,1,0:T(8,128)(2,1)} %all-to-all-done.3) | data formatting | bytes 8388608 | tf_op jit(solution)/shard_map/reshape | solution.py:102
  441.5 19.6 %all-to-all-done.4 = bf16[128,16,896]{2,1,0:T(8,128)(2,1)} async-done(((bf16[128,16,896]{2,1,0:T(8,128)(2,1)}), bf16[128,16,896]{2,1,0:T(8,128)(2,1)}, u32[]{:S(2)}, u32[]{:S(2)}) %all-to-all-start.4) | async-done | bytes 3670048 | tf_op jit(solution)/shard_map/all_to_all | solution.py:67
  (125 shorter events, 121.0 us)
Async XLA Ops:
  0.6 4.6 copy-start.16
  0.6 4.6 copy-start.8
  1.8 3.8 copy-start.9
  3.2 1.0 copy-start.13
  23.8 87.3 %all-to-all-start = ((bf16[128,32,768]{2,1,0:T(8,128)(2,1)}), bf16[128,32,768]{2,1,0:T(8,128)(2,1)}, u32[]{:S(2)}, u32[]{:S(2)}) async-start(bf16[128,32,768]{2,1,0:T(8,128)(2,1)} %reshape.300), calls=%async_computation | async-start | bytes 12582912 | tf_op jit(solution)/shard_map/all_to_all | solution.py:67
  111.1 105.5 %all-to-all-start.1 = ((bf16[128,32,1024]{2,1,0:T(8,128)(2,1)}), bf16[128,32,1024]{2,1,0:T(8,128)(2,1)}, u32[]{:S(2)}, u32[]{:S(2)}) async-start(bf16[128,32,1024]{2,1,0:T(8,128)(2,1)} %reshape.302), calls=%async_computation.1 | async-start | bytes 16777216 | tf_op jit(solution)/shard_map/all_to_all | solution.py:67
  151.7 6.9 %copy-start.4 = (bf16[384,4096]{1,0:T(8,128)(2,1)S(1)}, bf16[384,4096]{1,0:T(8,128)(2,1)}, u32[]{:S(2)}) copy-start(bf16[384,4096]{1,0:T(8,128)(2,1)} %reshape.303) | copy-start | bytes 9437188
  151.7 6.9 %copy-start.17 = (bf16[1,512,4096]{2,1,0:T(8,128)(2,1)S(1)}, bf16[1,512,4096]{2,1,0:T(8,128)(2,1)}, u32[]{:S(2)}) copy-start(bf16[1,512,4096]{2,1,0:T(8,128)(2,1)} %param.15) | copy-start | bytes 12582916
  216.7 124.6 %all-to-all-start.2 = ((bf16[128,48,768]{2,1,0:T(8,128)(2,1)}), bf16[128,48,768]{2,1,0:T(8,128)(2,1)}, u32[]{:S(2)}, u32[]{:S(2)}) async-start(bf16[128,48,768]{2,1,0:T(8,128)(2,1)} %pad_maximum_fusion), calls=%async_computation.2 | async-start | bytes 18874368 | tf_op jit(solution)/shard_map/all_to_all | solution.py:67
  248.1 8.4 %copy-start.3 = (bf16[512,4096]{1,0:T(8,128)(2,1)S(1)}, bf16[512,4096]{1,0:T(8,128)(2,1)}, u32[]{:S(2)}) copy-start(bf16[512,4096]{1,0:T(8,128)(2,1)} %reshape.308) | copy-start | bytes 12582916
  248.1 8.4 %copy-start.18 = (bf16[1,512,4096]{2,1,0:T(8,128)(2,1)S(1)}, bf16[1,512,4096]{2,1,0:T(8,128)(2,1)}, u32[]{:S(2)}) copy-start(bf16[1,512,4096]{2,1,0:T(8,128)(2,1)} %param.15) | copy-start | bytes 12582916
  341.3 65.4 %all-to-all-start.3 = ((bf16[128,16,1024]{2,1,0:T(8,128)(2,1)}), bf16[128,16,1024]{2,1,0:T(8,128)(2,1)}, u32[]{:S(2)}, u32[]{:S(2)}) async-start(bf16[128,16,1024]{2,1,0:T(8,128)(2,1)} %reshape.310), calls=%async_computation.3 | async-start | bytes 8388608 | tf_op jit(solution)/shard_map/all_to_all | solution.py:67
  372.3 6.9 %copy-start.5 = (bf16[384,4096]{1,0:T(8,128)(2,1)S(1)}, bf16[384,4096]{1,0:T(8,128)(2,1)}, u32[]{:S(2)}) copy-start(bf16[384,4096]{1,0:T(8,128)(2,1)} %reshape.311) | copy-start | bytes 9437188
  372.3 6.9 %copy-start.19 = (bf16[1,512,4096]{2,1,0:T(8,128)(2,1)S(1)}, bf16[1,512,4096]{2,1,0:T(8,128)(2,1)}, u32[]{:S(2)}) copy-start(bf16[1,512,4096]{2,1,0:T(8,128)(2,1)} %param.15) | copy-start | bytes 12582916
  404.0 10.6 %copy-start.11 = (s32[1024]{0:T(1024)S(1)}, s32[1024]{0:T(1024)}, u32[]{:S(2)}) copy-start(s32[1024]{0:T(1024)} %copy-done.10) | copy-start | bytes 12292
  404.0 10.7 %copy-start.12 = (s32[128,8]{0,1:T(8,128)S(1)}, s32[128,8]{0,1:T(8,128)}, u32[]{:S(2)}) copy-start(s32[128,8]{0,1:T(8,128)} %param.11) | copy-start | bytes 12292
  404.0 11.0 %copy-start.15 = (f32[128,8]{0,1:T(8,128)S(1)}, f32[128,8]{0,1:T(8,128)}, u32[]{:S(2)}) copy-start(f32[128,8]{0,1:T(8,128)} %param.10) | copy-start | bytes 12292
  406.6 54.5 %all-to-all-start.4 = ((bf16[128,16,896]{2,1,0:T(8,128)(2,1)}), bf16[128,16,896]{2,1,0:T(8,128)(2,1)}, u32[]{:S(2)}, u32[]{:S(2)}) async-start(bf16[128,16,896]{2,1,0:T(8,128)(2,1)} %pad_maximum_fusion.1), calls=%async_computation.4 | async-start | bytes 7340032 | tf_op jit(solution)/shard_map/all_to_all | solution.py:67
  423.9 1.7 copy-start.7
  435.2 3.4 copy-start
  435.2 4.1 copy-start.1
  466.7 7.0 %copy-start.14 = (s32[1024]{0:T(1024)S(1)}, s32[1024]{0:T(1024)}, u32[]{:S(2)}) copy-start(s32[1024]{0:T(1024)} %copy-done.13) | copy-start | bytes 12292
  466.7 8.6 %copy-start.6 = (f32[128,384]{1,0:T(8,128)S(1)}, f32[128,384]{1,0:T(8,128)}, u32[]{:S(2)}) copy-start(f32[128,384]{1,0:T(8,128)} %select_reduce_fusion.3) | copy-start | bytes 589828
  475.3 1.6 copy-start.2
  (1 other events, 0.6 us)

commit v3 on v2

--- a/solution.py
+++ b/solution.py
@@ -5,7 +5,7 @@
 
 STRATA = 8
 LEVELS = 64
-CHUNK_SIZES = (3, 4, 3)
+CHUNK_SIZES = (2, 6, 2)
 
 
 def expert_grads(inputs, upstream, weight_in, weight_out):

time: 488 us -> 491 us (level)
  waiting for transfers between devices: 173 us -> 195 us
  starting transfers between devices: 49 us -> 42 us
  other arithmetic: 17.4 us -> 12.1 us
    all_to_all x5, waiting for transfers between devices: 173 us -> 195 us  [exchange(): return lax.all_to_all(part, axes, 0, 0, tiled=True)]
    all_to_all x5, starting transfers between devices: 49 us -> 42 us  [exchange(): return lax.all_to_all(part, axes, 0, 0, tiled=True)]
  transfers between devices with their start and end apart: 5 -> 5, of which waited for: 5 -> 4; matrix products, arithmetic and copies ran while one was open for 45% -> 44% of each run, Pallas kernels for 0% -> 0%
where the time goes in v3:
time: 491 us; the launch traced here: 482 us
  waiting for transfers between devices  195 us (40%)
  local copies, waits for them, and re-layouts  162 us (33%)
  matrix products  69 us (14%)
  starting transfers between devices  42 us (9%)
  other arithmetic  12.1 us (2%)
    all_to_all x5, waiting for transfers between devices, exchange(): return lax.all_to_all(part, axes, 0, 0, tiled=True)  195 us
    all_to_all x5, starting transfers between devices, exchange(): return lax.all_to_all(part, axes, 0, 0, tiled=True)  42 us
    reshape x3, local copies, waits for them, and re-layouts, send_of(): sources[index].reshape(device_count, 2 * rows, sizes[c] * width // rows)  37.7 us
    dot_general x3, matrix products, expert_grads(): jnp.dot(stacked, weight_in.T, preferred_element_type=jnp.float32)  26.9 us
    dot_general x3, matrix products, expert_grads(): projected = jnp.dot(inputs, weight_in, preferred_element_type=jnp.float32)  24.3 us
    reshape x3, local copies, waits for them, and re-layouts, compute(): arrived[:, :rows].reshape(device_count * n, width)  20.7 us
    gather x3, local copies, waits for them, and re-layouts, send_of(): sources[index].reshape(device_count, 2 * rows, sizes[c] * width // rows)  18.3 us
    reshape x3, local copies, waits for them, and re-layouts, combine(): home = home.reshape(device_count * n, width)  18.1 us
  transfers between devices with their start and end apart: 5, of which 4 were waited for; matrix products, arithmetic and copies ran while one was open for 44% of the time, Pallas kernels for 0%

profile of v3, /device:TPU:1, one launch (start us, length us, event | category | flops | bytes accessed | tf_op | source)
XLA Modules:
  0.0 482.3 jit_solution(16659042669910733744)
XLA Ops:
  10.3 7.4 %reshape.300 = bf16[128,32,512]{2,1,0:T(8,128)(2,1)} reshape(bf16[512,4096]{1,0:T(8,128)(2,1)} %gather_fusion) | data formatting | bytes 8388608 | tf_op jit(solution)/shard_map/reshape | solution.py:74
  17.7 11.9 %all-to-all-start = ((bf16[128,32,512]{2,1,0:T(8,128)(2,1)}), bf16[128,32,512]{2,1,0:T(8,128)(2,1)}, u32[]{:S(2)}, u32[]{:S(2)}) async-start(bf16[128,32,512]{2,1,0:T(8,128)(2,1)} %reshape.300), calls=%async_computation | async-start | bytes 8388608 | tf_op jit(solution)/shard_map/all_to_all | solution.py:67
  30.1 9.6 %gather_fusion.1 = bf16[1536,4096]{1,0:T(8,128)(2,1)} fusion(bf16[258,4096]{1,0:T(8,128)(2,1)S(1)} %pad_maximum_fusion.2, s32[2048]{0:T(1024)S(1)} %pad_clamp_fusion), kind=kCustom, calls=%fused_computation.1 | custom fusion | bytes 25171968 | tf_op jit(solution)/shard_map/gather | solution.py:74
  39.7 22.9 %reshape.302 = bf16[128,32,1536]{2,1,0:T(8,128)(2,1)} reshape(bf16[1536,4096]{1,0:T(8,128)(2,1)} %gather_fusion.1) | data formatting | bytes 25165824 | tf_op jit(solution)/shard_map/reshape | solution.py:74
  62.6 19.4 %all-to-all-done = bf16[128,32,512]{2,1,0:T(8,128)(2,1)} async-done(((bf16[128,32,512]{2,1,0:T(8,128)(2,1)}), bf16[128,32,512]{2,1,0:T(8,128)(2,1)}, u32[]{:S(2)}, u32[]{:S(2)}) %all-to-all-start) | async-done | bytes 4194336 | tf_op jit(solution)/shard_map/all_to_all | solution.py:67
  92.0 7.4 %reshape.307 = bf16[128,32,512]{2,1,0:T(8,128)(2,1)} reshape(bf16[512,4096]{1,0:T(8,128)(2,1)} %gather_fusion.2) | data formatting | bytes 8388608 | tf_op jit(solution)/shard_map/reshape | solution.py:74
  109.9 6.5 %fusion.10 = f32[256,1024]{1,0:T(8,128)S(1)} fusion(bf16[256,4096]{1,0:T(8,128)(2,1)} %reshape.304, bf16[1,4096,1024]{2,1,0:T(8,128)(2,1)} %param.14), kind=kOutput, calls=%fused_computation.13 | convolution fusion | flops 2147483648 | bytes 11534336 | tf_op jit(solution)/shard_map/dot_general | solution.py:13
  118.0 7.2 %fusion.15 = bf16[256,4096]{1,0:T(8,128)(2,1)} fusion(bf16[1,4096,1024]{2,1,0:T(8,128)(2,1)} %param.14, bf16[256,512]{1,0:T(8,128)(2,1)S(1)} %get-tuple-element.42, bf16[256,512]{1,0:T(8,128)(2,1)S(1)} %get-tuple-element.43), kind=kOutput, calls=%fused_computation.21 | convolution fusion | flops 2149580800 | bytes 11010048 | tf_op jit(solution)/shard_map/dot_general | solution.py:24
  133.4 126.0 %all-to-all-done.1 = bf16[128,32,1536]{2,1,0:T(8,128)(2,1)} async-done(((bf16[128,32,1536]{2,1,0:T(8,128)(2,1)}), bf16[128,32,1536]{2,1,0:T(8,128)(2,1)}, u32[]{:S(2)}, u32[]{:S(2)}) %all-to-all-start.1) | async-done | bytes 12582944 | tf_op jit(solution)/shard_map/all_to_all | solution.py:67
  259.4 8.8 %all-to-all-start.2 = ((bf16[128,48,512]{2,1,0:T(8,128)(2,1)}), bf16[128,48,512]{2,1,0:T(8,128)(2,1)}, u32[]{:S(2)}, u32[]{:S(2)}) async-start(bf16[128,48,512]{2,1,0:T(8,128)(2,1)} %pad_maximum_fusion), calls=%async_computation.2 | async-start | bytes 12582912 | tf_op jit(solution)/shard_map/all_to_all | solution.py:67
  268.3 10.6 %fusion.70 = (bf16[128,16,1536]{2,1,0:T(8,128)(2,1)}, bf16[128,16,1536]{2,1,0:T(8,128)(2,1)}) fusion(bf16[128,32,1536]{2,1,0:T(8,128)(2,1)} %all-to-all-done.1), kind=kLoop, calls=%fused_computation.139 | loop fusion | bytes 25165824 | tf_op jit(solution)/shard_map/slice | solution.py:79
  278.9 12.3 %reshape.309 = bf16[768,4096]{1,0:T(8,128)(2,1)} reshape(bf16[128,16,1536]{2,1,0:T(8,128)(2,1)} %get-tuple-element.28) | data formatting | bytes 12582912 | tf_op jit(solution)/shard_map/reshape | solution.py:79
  291.2 12.3 %reshape.308 = bf16[768,4096]{1,0:T(8,128)(2,1)} reshape(bf16[128,16,1536]{2,1,0:T(8,128)(2,1)} %get-tuple-element.29) | data formatting | bytes 12582912 | tf_op jit(solution)/shard_map/reshape | solution.py:80
  303.5 11.3 %fusion.6 = f32[768,1024]{0,1:T(8,128)S(1)} fusion(bf16[768,4096]{1,0:T(8,128)(2,1)} %reshape.309, bf16[1,4096,1024]{2,1,0:T(8,128)(2,1)} %param.14), kind=kOutput, calls=%fused_computation.9 | convolution fusion | flops 6442450944 | bytes 17825792 | tf_op jit(solution)/shard_map/dot_general | solution.py:13
  319.0 12.4 %fusion.12 = bf16[768,4096]{1,0:T(8,128)(2,1)} fusion(bf16[1,4096,1024]{2,1,0:T(8,128)(2,1)} %param.14, bf16[768,512]{0,1:T(8,128)(2,1)S(1)} %get-tuple-element.34, bf16[768,512]{0,1:T(8,128)(2,1)S(1)} %get-tuple-element.35), kind=kOutput, calls=%fused_computation.15 | convolution fusion | flops 6448742400 | bytes 16252928 | tf_op jit(solution)/shard_map/dot_general | solution.py:24
  331.4 12.3 %reshape.310 = bf16[128,16,1536]{2,1,0:T(8,128)(2,1)} reshape(bf16[768,4096]{1,0:T(8,128)(2,1)} %fusion.12) | data formatting | bytes 12582912 | tf_op jit(solution)/shard_map/reshape | solution.py:84
  343.7 10.2 %all-to-all-start.3 = ((bf16[128,16,1536]{2,1,0:T(8,128)(2,1)}), bf16[128,16,1536]{2,1,0:T(8,128)(2,1)}, u32[]{:S(2)}, u32[]{:S(2)}) async-start(bf16[128,16,1536]{2,1,0:T(8,128)(2,1)} %reshape.310), calls=%async_computation.3 | async-start | bytes 12582912 | tf_op jit(solution)/shard_map/all_to_all | solution.py:67
  354.8 5.6 %fusion.71 = (bf16[128,16,512]{2,1,0:T(8,128)(2,1)}, bf16[128,16,512]{2,1,0:T(8,128)(2,1)}, bf16[128,16,512]{2,1,0:T(8,128)(2,1)S(1)}) fusion(bf16[128,48,512]{2,1,0:T(8,128)(2,1)} %all-to-all-done.2), kind=kLoop, calls=%fused_computation.140 | loop fusion | bytes 12582912 | tf_op jit(solution)/shard_map/slice | solution.py:163
  367.0 6.5 %fusion.2 = f32[256,1024]{1,0:T(8,128)S(1)} fusion(bf16[256,4096]{1,0:T(8,128)(2,1)} %reshape.312, bf16[1,4096,1024]{2,1,0:T(8,128)(2,1)} %param.14), kind=kOutput, calls=%fused_computation.5 | convolution fusion | flops 2147483648 | bytes 11534336 | tf_op jit(solution)/shard_map/dot_general | solution.py:13
  375.0 7.2 %fusion.18 = bf16[256,4096]{1,0:T(8,128)(2,1)} fusion(bf16[1,4096,1024]{2,1,0:T(8,128)(2,1)} %param.14, bf16[256,512]{1,0:T(8,128)(2,1)S(1)} %get-tuple-element.40, bf16[256,512]{1,0:T(8,128)(2,1)S(1)} %get-tuple-element.38), kind=kOutput, calls=%fused_computation.22 | convolution fusion | flops 2149580800 | bytes 11010048 | tf_op jit(solution)/shard_map/dot_general | solution.py:24
  387.6 41.7 %all-to-all-done.3 = bf16[128,16,1536]{2,1,0:T(8,128)(2,1)} async-done(((bf16[128,16,1536]{2,1,0:T(8,128)(2,1)}), bf16[128,16,1536]{2,1,0:T(8,128)(2,1)}, u32[]{:S(2)}, u32[]{:S(2)}) %all-to-all-start.3) | async-done | bytes 6291488 | tf_op jit(solution)/shard_map/all_to_all | solution.py:67
  429.3 5.7 %all-to-all-start.4 = ((bf16[128,16,640]{2,1,0:T(8,128)(2,1)}), bf16[128,16,640]{2,1,0:T(8,128)(2,1)}, u32[]{:S(2)}, u32[]{:S(2)}) async-start(bf16[128,16,640]{2,1,0:T(8,128)(2,1)} %pad_maximum_fusion.1), calls=%async_computation.4 | async-start | bytes 5242880 | tf_op jit(solution)/shard_map/all_to_all | solution.py:67
  441.6 12.3 %reshape.316 = bf16[768,4096]{1,0:T(8,128)(2,1)} reshape(bf16[128,16,1536]{2,1,0:T(8,128)(2,1)} %all-to-all-done.3) | data formatting | bytes 12582912 | tf_op jit(solution)/shard_map/reshape | solution.py:102
  462.0 7.8 %all-to-all-done.4 = bf16[128,16,640]{2,1,0:T(8,128)(2,1)} async-done(((bf16[128,16,640]{2,1,0:T(8,128)(2,1)}), bf16[128,16,640]{2,1,0:T(8,128)(2,1)}, u32[]{:S(2)}, u32[]{:S(2)}) %all-to-all-start.4) | async-done | bytes 2621472 | tf_op jit(solution)/shard_map/all_to_all | solution.py:67
  (120 shorter events, 84.7 us)
Async XLA Ops:
  0.6 4.6 copy-start.14
  0.6 4.6 copy-start.6
  1.8 3.7 copy-start.7
  2.6 0.6 copy-start.8
  3.2 1.0 copy-start.11
  17.7 64.3 %all-to-all-start = ((bf16[128,32,512]{2,1,0:T(8,128)(2,1)}), bf16[128,32,512]{2,1,0:T(8,128)(2,1)}, u32[]{:S(2)}, u32[]{:S(2)}) async-start(bf16[128,32,512]{2,1,0:T(8,128)(2,1)} %reshape.300), calls=%async_computation | async-start | bytes 8388608 | tf_op jit(solution)/shard_map/all_to_all | solution.py:67
  81.9 177.5 %all-to-all-start.1 = ((bf16[128,32,1536]{2,1,0:T(8,128)(2,1)}), bf16[128,32,1536]{2,1,0:T(8,128)(2,1)}, u32[]{:S(2)}, u32[]{:S(2)}) async-start(bf16[128,32,1536]{2,1,0:T(8,128)(2,1)} %reshape.302), calls=%async_computation.1 | async-start | bytes 25165824 | tf_op jit(solution)/shard_map/all_to_all | solution.py:67
  109.9 6.5 %copy-start.4 = (bf16[256,4096]{1,0:T(8,128)(2,1)S(1)}, bf16[256,4096]{1,0:T(8,128)(2,1)}, u32[]{:S(2)}) copy-start(bf16[256,4096]{1,0:T(8,128)(2,1)} %reshape.303) | copy-start | bytes 6291460
  109.9 6.5 %copy-start.15 = (bf16[1,512,4096]{2,1,0:T(8,128)(2,1)S(1)}, bf16[1,512,4096]{2,1,0:T(8,128)(2,1)}, u32[]{:S(2)}) copy-start(bf16[1,512,4096]{2,1,0:T(8,128)(2,1)} %param.15) | copy-start | bytes 12582916
  259.4 84.3 %all-to-all-start.2 = ((bf16[128,48,512]{2,1,0:T(8,128)(2,1)}), bf16[128,48,512]{2,1,0:T(8,128)(2,1)}, u32[]{:S(2)}, u32[]{:S(2)}) async-start(bf16[128,48,512]{2,1,0:T(8,128)(2,1)} %pad_maximum_fusion), calls=%async_computation.2 | async-start | bytes 12582912 | tf_op jit(solution)/shard_map/all_to_all | solution.py:67
  303.5 11.3 %copy-start.3 = (bf16[768,4096]{1,0:T(8,128)(2,1)S(1)}, bf16[768,4096]{1,0:T(8,128)(2,1)}, u32[]{:S(2)}) copy-start(bf16[768,4096]{1,0:T(8,128)(2,1)} %reshape.308) | copy-start | bytes 18874372
  303.5 11.3 %copy-start.16 = (bf16[1,512,4096]{2,1,0:T(8,128)(2,1)S(1)}, bf16[1,512,4096]{2,1,0:T(8,128)(2,1)}, u32[]{:S(2)}) copy-start(bf16[1,512,4096]{2,1,0:T(8,128)(2,1)} %param.15) | copy-start | bytes 12582916
  343.7 10.2 %copy-start.9 = (s32[1024]{0:T(1024)S(1)}, s32[1024]{0:T(1024)}, u32[]{:S(2)}) copy-start(s32[1024]{0:T(1024)} %copy-done.8) | copy-start | bytes 12292
  343.7 10.3 %copy-start.10 = (s32[128,8]{0,1:T(8,128)S(1)}, s32[128,8]{0,1:T(8,128)}, u32[]{:S(2)}) copy-start(s32[128,8]{0,1:T(8,128)} %param.11) | copy-start | bytes 12292
  343.7 10.5 %copy-start.13 = (f32[128,8]{0,1:T(8,128)S(1)}, f32[128,8]{0,1:T(8,128)}, u32[]{:S(2)}) copy-start(f32[128,8]{0,1:T(8,128)} %param.10) | copy-start | bytes 12292
  343.7 85.6 %all-to-all-start.3 = ((bf16[128,16,1536]{2,1,0:T(8,128)(2,1)}), bf16[128,16,1536]{2,1,0:T(8,128)(2,1)}, u32[]{:S(2)}, u32[]{:S(2)}) async-start(bf16[128,16,1536]{2,1,0:T(8,128)(2,1)} %reshape.310), calls=%async_computation.3 | async-start | bytes 12582912 | tf_op jit(solution)/shard_map/all_to_all | solution.py:67
  367.0 6.5 %copy-start.5 = (bf16[256,4096]{1,0:T(8,128)(2,1)S(1)}, bf16[256,4096]{1,0:T(8,128)(2,1)}, u32[]{:S(2)}) copy-start(bf16[256,4096]{1,0:T(8,128)(2,1)} %reshape.311) | copy-start | bytes 6291460
  367.0 6.5 %copy-start.17 = (bf16[1,512,4096]{2,1,0:T(8,128)(2,1)S(1)}, bf16[1,512,4096]{2,1,0:T(8,128)(2,1)}, u32[]{:S(2)}) copy-start(bf16[1,512,4096]{2,1,0:T(8,128)(2,1)} %param.15) | copy-start | bytes 12582916
  429.3 40.6 %all-to-all-start.4 = ((bf16[128,16,640]{2,1,0:T(8,128)(2,1)}), bf16[128,16,640]{2,1,0:T(8,128)(2,1)}, u32[]{:S(2)}, u32[]{:S(2)}) async-start(bf16[128,16,640]{2,1,0:T(8,128)(2,1)} %pad_maximum_fusion.1), calls=%async_computation.4 | async-start | bytes 5242880 | tf_op jit(solution)/shard_map/all_to_all | solution.py:67
  453.9 4.6 copy-start
  458.5 1.6 copy-start.2
  472.9 4.3 copy-start.12
  478.8 1.6 copy-start.1

commit v4 on v2

--- a/solution.py
+++ b/solution.py
@@ -41,10 +41,9 @@
     upstream = (cotangent.astype(jnp.float32) * loss_weight[:, None]).astype(jnp.bfloat16)
     chosen = experts.reshape(-1)
     pair_count = chosen.shape[0]
-    onehot = (chosen[:, None] == jnp.arange(device_count, dtype=jnp.int32)[None, :]).astype(
-        jnp.int32
-    )
-    ranking = jnp.sum((jnp.cumsum(onehot, axis=0) - 1) * onehot, axis=1)
+    order_of = jnp.arange(pair_count, dtype=jnp.int32)
+    earlier = (chosen[None, :] == chosen[:, None]) & (order_of[None, :] < order_of[:, None])
+    ranking = jnp.sum(earlier.astype(jnp.int32), axis=1)
     placed = chosen * capacity + ranking
     holder = placed[None, :] == jnp.arange(device_count * capacity, dtype=jnp.int32)[:, None]
     token_index = jnp.min(

time: 488 us -> 489 us (level)
  no operation moved by 1% of the time
where the time goes in v4:
time: 489 us; the launch traced here: 480 us
  waiting for transfers between devices  173 us (35%)
  local copies, waits for them, and re-layouts  166 us (34%)
  matrix products  71.2 us (15%)
  starting transfers between devices  49 us (10%)
  other arithmetic  19.1 us (4%)
    all_to_all x5, waiting for transfers between devices, exchange(): return lax.all_to_all(part, axes, 0, 0, tiled=True)  173 us
    all_to_all x5, starting transfers between devices, exchange(): return lax.all_to_all(part, axes, 0, 0, tiled=True)  49 us
    reshape x3, local copies, waits for them, and re-layouts, send_of(): sources[index].reshape(device_count, 2 * rows, sizes[c] * width // rows)  38.3 us
    dot_general x3, matrix products, expert_grads(): jnp.dot(stacked, weight_in.T, preferred_element_type=jnp.float32)  30.4 us
    dot_general x3, matrix products, expert_grads(): projected = jnp.dot(inputs, weight_in, preferred_element_type=jnp.float32)  22.2 us
    reshape x3, local copies, waits for them, and re-layouts, compute(): arrived[:, :rows].reshape(device_count * n, width)  21 us
    gather x3, local copies, waits for them, and re-layouts, send_of(): sources[index].reshape(device_count, 2 * rows, sizes[c] * width // rows)  19.2 us
    reshape x3, local copies, waits for them, and re-layouts, combine(): home = home.reshape(device_count * n, width)  18.8 us
  transfers between devices with their start and end apart: 5, of which 5 were waited for; matrix products, arithmetic and copies ran while one was open for 45% of the time, Pallas kernels for 0%

profile of v4, /device:TPU:1, one launch (start us, length us, event | category | flops | bytes accessed | tf_op | source)
XLA Modules:
  0.0 480.5 jit_solution(10097504404020590625)
XLA Ops:
  13.1 12.2 %reshape.282 = bf16[128,32,768]{2,1,0:T(8,128)(2,1)} reshape(bf16[768,4096]{1,0:T(8,128)(2,1)} %gather_fusion) | data formatting | bytes 12582912 | tf_op jit(solution)/shard_map/reshape | solution.py:73
  25.3 11.9 %all-to-all-start = ((bf16[128,32,768]{2,1,0:T(8,128)(2,1)}), bf16[128,32,768]{2,1,0:T(8,128)(2,1)}, u32[]{:S(2)}, u32[]{:S(2)}) async-start(bf16[128,32,768]{2,1,0:T(8,128)(2,1)} %reshape.282), calls=%async_computation | async-start | bytes 12582912 | tf_op jit(solution)/shard_map/all_to_all | solution.py:66
  37.6 7.8 %gather_fusion.1 = bf16[1024,4096]{1,0:T(8,128)(2,1)} fusion(bf16[258,4096]{1,0:T(8,128)(2,1)S(1)} %pad_maximum_fusion.2, s32[1024]{0:T(1024)S(1)} %broadcast_clamp_fusion), kind=kCustom, calls=%fused_computation.1 | custom fusion | bytes 16781312 | tf_op jit(solution)/shard_map/gather | solution.py:73
  45.4 13.9 %reshape.284 = bf16[128,32,1024]{2,1,0:T(8,128)(2,1)} reshape(bf16[1024,4096]{1,0:T(8,128)(2,1)} %gather_fusion.1) | data formatting | bytes 16777216 | tf_op jit(solution)/shard_map/reshape | solution.py:73
  59.3 53.3 %all-to-all-done = bf16[128,32,768]{2,1,0:T(8,128)(2,1)} async-done(((bf16[128,32,768]{2,1,0:T(8,128)(2,1)}), bf16[128,32,768]{2,1,0:T(8,128)(2,1)}, u32[]{:S(2)}, u32[]{:S(2)}) %all-to-all-start) | async-done | bytes 6291488 | tf_op jit(solution)/shard_map/all_to_all | solution.py:66
  124.6 12.2 %reshape.289 = bf16[128,32,768]{2,1,0:T(8,128)(2,1)} reshape(bf16[768,4096]{1,0:T(8,128)(2,1)} %gather_fusion.2) | data formatting | bytes 12582912 | tf_op jit(solution)/shard_map/reshape | solution.py:73
  153.2 6.9 %fusion.10 = f32[384,1024]{1,0:T(8,128)S(1)} fusion(bf16[384,4096]{1,0:T(8,128)(2,1)} %reshape.286, bf16[1,4096,1024]{2,1,0:T(8,128)(2,1)} %param.14), kind=kOutput, calls=%fused_computation.14 | convolution fusion | flops 3221225472 | bytes 13107200 | tf_op jit(solution)/shard_map/dot_general | solution.py:13
  162.3 10.3 %fusion.15 = bf16[384,4096]{1,0:T(8,128)(2,1)} fusion(bf16[1,4096,1024]{2,1,0:T(8,128)(2,1)} %param.14, bf16[384,512]{1,0:T(8,128)(2,1)S(1)} %get-tuple-element.42, bf16[384,512]{1,0:T(8,128)(2,1)S(1)} %get-tuple-element.43), kind=kOutput, calls=%fused_computation.17 | convolution fusion | flops 3224371200 | bytes 12320768 | tf_op jit(solution)/shard_map/dot_general | solution.py:24
  178.4 7.0 %pad_maximum_fusion = bf16[128,48,768]{2,1,0:T(8,128)(2,1)} fusion(bf16[128,32,768]{2,1,0:T(8,128)(2,1)} %reshape.289, bf16[128,16,768]{2,1,0:T(8,128)(2,1)S(1)} %reshape.287), kind=kLoop, calls=%fused_computation.3 | loop fusion | flops 18874368 | bytes 18874368 | tf_op jit(solution)/shard_map/concatenate | solution.py:137
  185.4 32.6 %all-to-all-done.1 = bf16[128,32,1024]{2,1,0:T(8,128)(2,1)} async-done(((bf16[128,32,1024]{2,1,0:T(8,128)(2,1)}), bf16[128,32,1024]{2,1,0:T(8,128)(2,1)}, u32[]{:S(2)}, u32[]{:S(2)}) %all-to-all-start.1) | async-done | bytes 8388640 | tf_op jit(solution)/shard_map/all_to_all | solution.py:66
  218.1 10.0 %all-to-all-start.2 = ((bf16[128,48,768]{2,1,0:T(8,128)(2,1)}), bf16[128,48,768]{2,1,0:T(8,128)(2,1)}, u32[]{:S(2)}, u32[]{:S(2)}) async-start(bf16[128,48,768]{2,1,0:T(8,128)(2,1)} %pad_maximum_fusion), calls=%async_computation.2 | async-start | bytes 18874368 | tf_op jit(solution)/shard_map/all_to_all | solution.py:66
  234.4 7.5 %reshape.291 = bf16[512,4096]{1,0:T(8,128)(2,1)} reshape(bf16[128,16,1024]{2,1,0:T(8,128)(2,1)} %get-tuple-element.31) | data formatting | bytes 8388608 | tf_op jit(solution)/shard_map/reshape | solution.py:78
  242.0 7.5 %reshape.290 = bf16[512,4096]{1,0:T(8,128)(2,1)} reshape(bf16[128,16,1024]{2,1,0:T(8,128)(2,1)} %get-tuple-element.32) | data formatting | bytes 8388608 | tf_op jit(solution)/shard_map/reshape | solution.py:79
  249.5 8.4 %fusion.6 = f32[512,1024]{0,1:T(8,128)S(1)} fusion(bf16[512,4096]{1,0:T(8,128)(2,1)} %reshape.291, bf16[1,4096,1024]{2,1,0:T(8,128)(2,1)} %param.14), kind=kOutput, calls=%fused_computation.10 | convolution fusion | flops 4294967296 | bytes 14680064 | tf_op jit(solution)/shard_map/dot_general | solution.py:13
  260.7 9.7 %fusion.12 = bf16[512,4096]{1,0:T(8,128)(2,1)} fusion(bf16[1,4096,1024]{2,1,0:T(8,128)(2,1)} %param.14, bf16[512,512]{0,1:T(8,128)(2,1)S(1)} %get-tuple-element.36, bf16[512,512]{0,1:T(8,128)(2,1)S(1)} %get-tuple-element.37), kind=kOutput, calls=%fused_computation.16 | convolution fusion | flops 4299161600 | bytes 13631488 | tf_op jit(solution)/shard_map/dot_general | solution.py:24
  270.4 7.5 %reshape.292 = bf16[128,16,1024]{2,1,0:T(8,128)(2,1)} reshape(bf16[512,4096]{1,0:T(8,128)(2,1)} %fusion.12) | data formatting | bytes 8388608 | tf_op jit(solution)/shard_map/reshape | solution.py:83
  277.9 64.8 %all-to-all-done.2 = bf16[128,48,768]{2,1,0:T(8,128)(2,1)} async-done(((bf16[128,48,768]{2,1,0:T(8,128)(2,1)}), bf16[128,48,768]{2,1,0:T(8,128)(2,1)}, u32[]{:S(2)}, u32[]{:S(2)}) %all-to-all-start.2) | async-done | bytes 9437216 | tf_op jit(solution)/shard_map/all_to_all | solution.py:66
  342.7 13.2 %all-to-all-start.3 = ((bf16[128,16,1024]{2,1,0:T(8,128)(2,1)}), bf16[128,16,1024]{2,1,0:T(8,128)(2,1)}, u32[]{:S(2)}, u32[]{:S(2)}) async-start(bf16[128,16,1024]{2,1,0:T(8,128)(2,1)} %reshape.292), calls=%async_computation.3 | async-start | bytes 8388608 | tf_op jit(solution)/shard_map/all_to_all | solution.py:66
  362.4 6.7 %reshape.294 = bf16[384,4096]{1,0:T(8,128)(2,1)} reshape(bf16[128,16,768]{2,1,0:T(8,128)(2,1)} %get-tuple-element.29) | data formatting | bytes 6291456 | tf_op jit(solution)/shard_map/reshape | solution.py:78
  373.8 6.9 %fusion.2 = f32[384,1024]{1,0:T(8,128)S(1)} fusion(bf16[384,4096]{1,0:T(8,128)(2,1)} %reshape.294, bf16[1,4096,1024]{2,1,0:T(8,128)(2,1)} %param.14), kind=kOutput, calls=%fused_computation.6 | convolution fusion | flops 3221225472 | bytes 13107200 | tf_op jit(solution)/shard_map/dot_general | solution.py:13
  382.9 10.4 %fusion.18 = bf16[384,4096]{1,0:T(8,128)(2,1)} fusion(bf16[1,4096,1024]{2,1,0:T(8,128)(2,1)} %param.14, bf16[384,512]{1,0:T(8,128)(2,1)S(1)} %get-tuple-element.40, bf16[384,512]{1,0:T(8,128)(2,1)S(1)} %get-tuple-element.38), kind=kOutput, calls=%fused_computation.18 | convolution fusion | flops 3224371200 | bytes 12320768 | tf_op jit(solution)/shard_map/dot_general | solution.py:24
  408.1 7.9 %all-to-all-start.4 = ((bf16[128,16,896]{2,1,0:T(8,128)(2,1)}), bf16[128,16,896]{2,1,0:T(8,128)(2,1)}, u32[]{:S(2)}, u32[]{:S(2)}) async-start(bf16[128,16,896]{2,1,0:T(8,128)(2,1)} %pad_maximum_fusion.1), calls=%async_computation.4 | async-start | bytes 7340032 | tf_op jit(solution)/shard_map/all_to_all | solution.py:66
  429.1 7.5 %reshape.298 = bf16[512,4096]{1,0:T(8,128)(2,1)} reshape(bf16[128,16,1024]{2,1,0:T(8,128)(2,1)} %all-to-all-done.3) | data formatting | bytes 8388608 | tf_op jit(solution)/shard_map/reshape | solution.py:101
  442.9 19.6 %all-to-all-done.4 = bf16[128,16,896]{2,1,0:T(8,128)(2,1)} async-done(((bf16[128,16,896]{2,1,0:T(8,128)(2,1)}), bf16[128,16,896]{2,1,0:T(8,128)(2,1)}, u32[]{:S(2)}, u32[]{:S(2)}) %all-to-all-start.4) | async-done | bytes 3670048 | tf_op jit(solution)/shard_map/all_to_all | solution.py:66
  (113 shorter events, 122.4 us)
Async XLA Ops:
  0.6 6.4 %copy-start.8 = (bf16[128,4096]{1,0:T(8,128)(2,1)S(1)}, bf16[128,4096]{1,0:T(8,128)(2,1)}, u32[]{:S(2)}) copy-start(bf16[128,4096]{1,0:T(8,128)(2,1)} %param.8) | copy-start | bytes 3145732
  2.1 0.6 copy-start.10
  2.1 1.6 copy-start.12
  25.3 87.3 %all-to-all-start = ((bf16[128,32,768]{2,1,0:T(8,128)(2,1)}), bf16[128,32,768]{2,1,0:T(8,128)(2,1)}, u32[]{:S(2)}, u32[]{:S(2)}) async-start(bf16[128,32,768]{2,1,0:T(8,128)(2,1)} %reshape.282), calls=%async_computation | async-start | bytes 12582912 | tf_op jit(solution)/shard_map/all_to_all | solution.py:66
  112.5 105.5 %all-to-all-start.1 = ((bf16[128,32,1024]{2,1,0:T(8,128)(2,1)}), bf16[128,32,1024]{2,1,0:T(8,128)(2,1)}, u32[]{:S(2)}, u32[]{:S(2)}) async-start(bf16[128,32,1024]{2,1,0:T(8,128)(2,1)} %reshape.284), calls=%async_computation.1 | async-start | bytes 16777216 | tf_op jit(solution)/shard_map/all_to_all | solution.py:66
  153.2 6.9 %copy-start.4 = (bf16[384,4096]{1,0:T(8,128)(2,1)S(1)}, bf16[384,4096]{1,0:T(8,128)(2,1)}, u32[]{:S(2)}) copy-start(bf16[384,4096]{1,0:T(8,128)(2,1)} %reshape.285) | copy-start | bytes 9437188
  153.2 6.9 %copy-start.15 = (bf16[1,512,4096]{2,1,0:T(8,128)(2,1)S(1)}, bf16[1,512,4096]{2,1,0:T(8,128)(2,1)}, u32[]{:S(2)}) copy-start(bf16[1,512,4096]{2,1,0:T(8,128)(2,1)} %param.15) | copy-start | bytes 12582916
  218.1 124.6 %all-to-all-start.2 = ((bf16[128,48,768]{2,1,0:T(8,128)(2,1)}), bf16[128,48,768]{2,1,0:T(8,128)(2,1)}, u32[]{:S(2)}, u32[]{:S(2)}) async-start(bf16[128,48,768]{2,1,0:T(8,128)(2,1)} %pad_maximum_fusion), calls=%async_computation.2 | async-start | bytes 18874368 | tf_op jit(solution)/shard_map/all_to_all | solution.py:66
  249.5 8.4 %copy-start.3 = (bf16[512,4096]{1,0:T(8,128)(2,1)S(1)}, bf16[512,4096]{1,0:T(8,128)(2,1)}, u32[]{:S(2)}) copy-start(bf16[512,4096]{1,0:T(8,128)(2,1)} %reshape.290) | copy-start | bytes 12582916
  249.5 8.4 %copy-start.16 = (bf16[1,512,4096]{2,1,0:T(8,128)(2,1)S(1)}, bf16[1,512,4096]{2,1,0:T(8,128)(2,1)}, u32[]{:S(2)}) copy-start(bf16[1,512,4096]{2,1,0:T(8,128)(2,1)} %param.15) | copy-start | bytes 12582916
  342.7 65.4 %all-to-all-start.3 = ((bf16[128,16,1024]{2,1,0:T(8,128)(2,1)}), bf16[128,16,1024]{2,1,0:T(8,128)(2,1)}, u32[]{:S(2)}, u32[]{:S(2)}) async-start(bf16[128,16,1024]{2,1,0:T(8,128)(2,1)} %reshape.292), calls=%async_computation.3 | async-start | bytes 8388608 | tf_op jit(solution)/shard_map/all_to_all | solution.py:66
  373.8 6.9 %copy-start.5 = (bf16[384,4096]{1,0:T(8,128)(2,1)S(1)}, bf16[384,4096]{1,0:T(8,128)(2,1)}, u32[]{:S(2)}) copy-start(bf16[384,4096]{1,0:T(8,128)(2,1)} %reshape.293) | copy-start | bytes 9437188
  373.8 6.9 %copy-start.17 = (bf16[1,512,4096]{2,1,0:T(8,128)(2,1)S(1)}, bf16[1,512,4096]{2,1,0:T(8,128)(2,1)}, u32[]{:S(2)}) copy-start(bf16[1,512,4096]{2,1,0:T(8,128)(2,1)} %param.15) | copy-start | bytes 12582916
  405.4 10.6 %copy-start.11 = (s32[1024]{0:T(1024)S(1)}, s32[1024]{0:T(1024)}, u32[]{:S(2)}) copy-start(s32[1024]{0:T(1024)} %copy-done.10) | copy-start | bytes 12292
  405.4 10.7 %copy-start.9 = (s32[128,8]{0,1:T(8,128)S(1)}, s32[128,8]{0,1:T(8,128)}, u32[]{:S(2)}) copy-start(s32[128,8]{0,1:T(8,128)} %param.11) | copy-start | bytes 12292
  405.4 10.9 %copy-start.14 = (f32[128,8]{0,1:T(8,128)S(1)}, f32[128,8]{0,1:T(8,128)}, u32[]{:S(2)}) copy-start(f32[128,8]{0,1:T(8,128)} %param.10) | copy-start | bytes 12292
  408.1 54.4 %all-to-all-start.4 = ((bf16[128,16,896]{2,1,0:T(8,128)(2,1)}), bf16[128,16,896]{2,1,0:T(8,128)(2,1)}, u32[]{:S(2)}, u32[]{:S(2)}) async-start(bf16[128,16,896]{2,1,0:T(8,128)(2,1)} %pad_maximum_fusion.1), calls=%async_computation.4 | async-start | bytes 7340032 | tf_op jit(solution)/shard_map/all_to_all | solution.py:66
  425.3 1.7 copy-start.7
  436.6 3.4 copy-start
  436.6 4.1 copy-start.1
  468.1 7.0 %copy-start.13 = (s32[1024]{0:T(1024)S(1)}, s32[1024]{0:T(1024)}, u32[]{:S(2)}) copy-start(s32[1024]{0:T(1024)} %copy-done.12) | copy-start | bytes 12292
  468.1 8.6 %copy-start.6 = (f32[128,384]{1,0:T(8,128)S(1)}, f32[128,384]{1,0:T(8,128)}, u32[]{:S(2)}) copy-start(f32[128,384]{1,0:T(8,128)} %select_reduce_fusion.3) | copy-start | bytes 589828
  476.7 1.6 copy-start.2

commit v5 on v2

--- a/solution.py
+++ b/solution.py
@@ -57,11 +57,13 @@
     weight_out = w_down[0]
     sizes = CHUNK_SIZES if sum(CHUNK_SIZES) == capacity else (capacity,)
     starts = [sum(sizes[:c]) for c in range(len(sizes))]
-    tiled = all((n * width) % (16 * 128) == 0 for n in sizes)
-    rows = 16 if tiled else 1
+    cols = 256 if all((n * width) % (16 * 256) == 0 for n in sizes) else width
+
+    def rows_of(n):
+        return n * width // cols
 
     def block_of(n):
-        return (device_count, rows, n * width // rows)
+        return (device_count, rows_of(n), cols)
 
     def exchange(part):
         return lax.all_to_all(part, axes, 0, 0, tiled=True)
@@ -71,13 +73,13 @@
     def send_of(c):
         index = token_index[:, starts[c] : starts[c] + sizes[c]]
         index = jnp.stack([index, index + (token_rows + 1)], axis=1).reshape(-1)
-        return sources[index].reshape(device_count, 2 * rows, sizes[c] * width // rows)
+        return sources[index].reshape(device_count, 2 * rows_of(sizes[c]), cols)
 
     def compute(c, arrived):
         n = sizes[c]
         row_grads, prob_grad = expert_grads(
-            arrived[:, :rows].reshape(device_count * n, width),
-            arrived[:, rows:].reshape(device_count * n, width),
+            arrived[:, : rows_of(n)].reshape(device_count * n, width),
+            arrived[:, rows_of(n) :].reshape(device_count * n, width),
             weight_in,
             weight_out,
         )
@@ -105,8 +107,8 @@
         )
 
     last = len(sizes) - 1
-    extra = rows * 128 if rows * 128 >= capacity else capacity
-    extra_cols = extra // rows
+    extra_rows = 16 if 16 * cols >= capacity else -(-capacity // cols)
+    extra = extra_rows * cols
 
     order = [((), (0,))]
     if last >= 1:
@@ -122,9 +124,9 @@
     def final_block():
         probs = jnp.concatenate([prob_parts[i] for i in range(len(sizes))], axis=1)
         probs = jnp.pad(probs, ((0, 0), (0, extra - capacity))).reshape(
-            device_count, rows, extra_cols
-        )
-        return jnp.concatenate([row_grads[last], probs], axis=2)
+            device_count, extra_rows, cols
+        )
+        return jnp.concatenate([row_grads[last], probs], axis=1)
 
     arrived = {}
     returned = {}
@@ -160,16 +162,17 @@
             grad_tokens = covered[1]
         offset = 0
         for n in backs:
-            returned[n] = done[:, offset : offset + rows] if len(backs) + len(sends) > 1 else done
-            offset += rows
+            height = rows_of(sizes[n]) + (extra_rows if n == last else 0)
+            returned[n] = done[:, offset : offset + height] if len(backs) + len(sends) > 1 else done
+            offset += height
         for n in sends:
-            arrived[n] = done[:, offset : offset + 2 * rows] if len(backs) + len(sends) > 1 else done
-            offset += 2 * rows
+            arrived[n] = done[:, offset : offset + 2 * rows_of(sizes[n])] if len(backs) + len(sends) > 1 else done
+            offset += 2 * rows_of(sizes[n])
     pending = returned[last]
-    row_cols = sizes[last] * width // rows
-    part = combine(last, pending[:, :, :row_cols])
+    row_count = rows_of(sizes[last])
+    part = combine(last, pending[:, :row_count])
     grad_tokens = part if grad_tokens is None else grad_tokens + part
-    home_probs = pending[:, :, row_cols:].reshape(device_count, extra)[:, :capacity].reshape(-1)
+    home_probs = pending[:, row_count:].reshape(device_count, extra)[:, :capacity].reshape(-1)
     pick = placed[:, None] == jnp.arange(device_count * capacity, dtype=jnp.int32)[None, :]
     grad_probs = jnp.sum(
         jnp.where(pick, home_probs.astype(jnp.float32)[None, :], 0.0), axis=1

time: 488 us -> 490 us (level)
  waiting for transfers between devices: 173 us -> 191 us
  local copies, waits for them, and re-layouts: 166 us -> 153 us
    all_to_all x5, waiting for transfers between devices: 173 us -> 191 us  [exchange(): return lax.all_to_all(part, axes, 0, 0, tiled=True)]
    reshape x9, local copies, waits for them, and re-layouts: 76 us -> 67.6 us  [the longest x3 34.3 us: send_of(): return sources[index].reshape(device_count, 2 * rows_of(sizes[c]), cols)]
  transfers between devices with their start and end apart: 5 -> 5, of which waited for: 5 -> 5; matrix products, arithmetic and copies ran while one was open for 45% -> 42% of each run, Pallas kernels for 0% -> 0%
where the time goes in v5:
time: 490 us; the launch traced here: 482 us
  waiting for transfers between devices  191 us (39%)
  local copies, waits for them, and re-layouts  153 us (31%)
  matrix products  71.1 us (15%)
  starting transfers between devices  46.4 us (9%)
  other arithmetic  18.2 us (4%)
    all_to_all x5, waiting for transfers between devices, exchange(): return lax.all_to_all(part, axes, 0, 0, tiled=True)  191 us
    all_to_all x5, starting transfers between devices, exchange(): return lax.all_to_all(part, axes, 0, 0, tiled=True)  46.4 us
    reshape x3, local copies, waits for them, and re-layouts, send_of(): return sources[index].reshape(device_count, 2 * rows_of(sizes[c]), cols)  34.3 us
    dot_general x3, matrix products, expert_grads(): jnp.dot(stacked, weight_in.T, preferred_element_type=jnp.float32)  30.4 us
    dot_general x3, matrix products, expert_grads(): projected = jnp.dot(inputs, weight_in, preferred_element_type=jnp.float32)  22.2 us
    gather x3, local copies, waits for them, and re-layouts, send_of(): return sources[index].reshape(device_count, 2 * rows_of(sizes[c]), cols)  19.2 us
    reshape x3, local copies, waits for them, and re-layouts, compute(): arrived[:, :rows_of(n)].reshape(device_count * n, width)  19.1 us
    reshape x3, local copies, waits for them, and re-layouts, combine(): home = home.reshape(device_count * n, width)  15.9 us
  transfers between devices with their start and end apart: 5, of which 5 were waited for; matrix products, arithmetic and copies ran while one was open for 42% of the time, Pallas kernels for 0%

profile of v5, /device:TPU:1, one launch (start us, length us, event | category | flops | bytes accessed | tf_op | source)
XLA Modules:
  0.0 481.9 jit_solution(13220362547391416905)
XLA Ops:
  11.6 10.4 %reshape.300 = bf16[128,96,256]{2,1,0:T(8,128)(2,1)} reshape(bf16[768,4096]{1,0:T(8,128)(2,1)} %gather_fusion) | data formatting | bytes 12582912 | tf_op jit(solution)/shard_map/reshape | solution.py:76
  22.0 11.9 %all-to-all-start = ((bf16[128,96,256]{2,1,0:T(8,128)(2,1)}), bf16[128,96,256]{2,1,0:T(8,128)(2,1)}, u32[]{:S(2)}, u32[]{:S(2)}) async-start(bf16[128,96,256]{2,1,0:T(8,128)(2,1)} %reshape.300), calls=%async_computation | async-start | bytes 12582912 | tf_op jit(solution)/shard_map/all_to_all | solution.py:69
  34.4 7.8 %gather_fusion.1 = bf16[1024,4096]{1,0:T(8,128)(2,1)} fusion(bf16[258,4096]{1,0:T(8,128)(2,1)S(1)} %pad_maximum_fusion.2, s32[1024]{0:T(1024)S(1)} %broadcast_clamp_fusion), kind=kCustom, calls=%fused_computation.1 | custom fusion | bytes 16781312 | tf_op jit(solution)/shard_map/gather | solution.py:76
  42.1 13.5 %reshape.302 = bf16[128,128,256]{2,1,0:T(8,128)(2,1)} reshape(bf16[1024,4096]{1,0:T(8,128)(2,1)} %gather_fusion.1) | data formatting | bytes 16777216 | tf_op jit(solution)/shard_map/reshape | solution.py:76
  55.6 53.7 %all-to-all-done = bf16[128,96,256]{2,1,0:T(8,128)(2,1)} async-done(((bf16[128,96,256]{2,1,0:T(8,128)(2,1)}), bf16[128,96,256]{2,1,0:T(8,128)(2,1)}, u32[]{:S(2)}, u32[]{:S(2)}) %all-to-all-start) | async-done | bytes 6291488 | tf_op jit(solution)/shard_map/all_to_all | solution.py:69
  109.3 6.0 %all-to-all-start.1 = ((bf16[128,128,256]{2,1,0:T(8,128)(2,1)}), bf16[128,128,256]{2,1,0:T(8,128)(2,1)}, u32[]{:S(2)}, u32[]{:S(2)}) async-start(bf16[128,128,256]{2,1,0:T(8,128)(2,1)} %reshape.302), calls=%async_computation.1 | async-start | bytes 16777216 | tf_op jit(solution)/shard_map/all_to_all | solution.py:69
  121.5 10.4 %reshape.307 = bf16[128,96,256]{2,1,0:T(8,128)(2,1)} reshape(bf16[768,4096]{1,0:T(8,128)(2,1)} %gather_fusion.2) | data formatting | bytes 12582912 | tf_op jit(solution)/shard_map/reshape | solution.py:76
  146.2 6.9 %fusion.10 = f32[384,1024]{1,0:T(8,128)S(1)} fusion(bf16[384,4096]{1,0:T(8,128)(2,1)} %reshape.304, bf16[1,4096,1024]{2,1,0:T(8,128)(2,1)} %param.14), kind=kOutput, calls=%fused_computation.14 | convolution fusion | flops 3221225472 | bytes 13107200 | tf_op jit(solution)/shard_map/dot_general | solution.py:13
  155.3 10.3 %fusion.15 = bf16[384,4096]{1,0:T(8,128)(2,1)} fusion(bf16[1,4096,1024]{2,1,0:T(8,128)(2,1)} %param.14, bf16[384,512]{1,0:T(8,128)(2,1)S(1)} %get-tuple-element.42, bf16[384,512]{1,0:T(8,128)(2,1)S(1)} %get-tuple-element.43), kind=kOutput, calls=%fused_computation.17 | convolution fusion | flops 3224371200 | bytes 12320768 | tf_op jit(solution)/shard_map/dot_general | solution.py:24
  169.8 7.0 %pad_maximum_fusion = bf16[128,144,256]{2,1,0:T(8,128)(2,1)} fusion(bf16[128,96,256]{2,1,0:T(8,128)(2,1)} %reshape.307, bf16[128,48,256]{2,1,0:T(8,128)(2,1)S(1)} %reshape.305), kind=kLoop, calls=%fused_computation.3 | loop fusion | flops 18874368 | bytes 18874368 | tf_op jit(solution)/shard_map/concatenate | solution.py:140
  176.9 38.1 %all-to-all-done.1 = bf16[128,128,256]{2,1,0:T(8,128)(2,1)} async-done(((bf16[128,128,256]{2,1,0:T(8,128)(2,1)}), bf16[128,128,256]{2,1,0:T(8,128)(2,1)}, u32[]{:S(2)}, u32[]{:S(2)}) %all-to-all-start.1) | async-done | bytes 8388640 | tf_op jit(solution)/shard_map/all_to_all | solution.py:69
  214.9 10.3 %all-to-all-start.2 = ((bf16[128,144,256]{2,1,0:T(8,128)(2,1)}), bf16[128,144,256]{2,1,0:T(8,128)(2,1)}, u32[]{:S(2)}, u32[]{:S(2)}) async-start(bf16[128,144,256]{2,1,0:T(8,128)(2,1)} %pad_maximum_fusion), calls=%async_computation.2 | async-start | bytes 18874368 | tf_op jit(solution)/shard_map/all_to_all | solution.py:69
  225.3 6.1 %fusion.72 = (bf16[128,64,256]{2,1,0:T(8,128)(2,1)}, bf16[128,64,256]{2,1,0:T(8,128)(2,1)}) fusion(bf16[128,128,256]{2,1,0:T(8,128)(2,1)} %all-to-all-done.1), kind=kLoop, calls=%fused_computation.140 | loop fusion | bytes 16777216 | tf_op jit(solution)/shard_map/slice | solution.py:81
  231.4 7.4 %reshape.309 = bf16[512,4096]{1,0:T(8,128)(2,1)} reshape(bf16[128,64,256]{2,1,0:T(8,128)(2,1)} %get-tuple-element.31) | data formatting | bytes 8388608 | tf_op jit(solution)/shard_map/reshape | solution.py:81
  238.8 7.4 %reshape.308 = bf16[512,4096]{1,0:T(8,128)(2,1)} reshape(bf16[128,64,256]{2,1,0:T(8,128)(2,1)} %get-tuple-element.32) | data formatting | bytes 8388608 | tf_op jit(solution)/shard_map/reshape | solution.py:82
  246.2 8.4 %fusion.6 = f32[512,1024]{0,1:T(8,128)S(1)} fusion(bf16[512,4096]{1,0:T(8,128)(2,1)} %reshape.309, bf16[1,4096,1024]{2,1,0:T(8,128)(2,1)} %param.14), kind=kOutput, calls=%fused_computation.10 | convolution fusion | flops 4294967296 | bytes 14680064 | tf_op jit(solution)/shard_map/dot_general | solution.py:13
  257.4 9.7 %fusion.12 = bf16[512,4096]{1,0:T(8,128)(2,1)} fusion(bf16[1,4096,1024]{2,1,0:T(8,128)(2,1)} %param.14, bf16[512,512]{0,1:T(8,128)(2,1)S(1)} %get-tuple-element.36, bf16[512,512]{0,1:T(8,128)(2,1)S(1)} %get-tuple-element.37), kind=kOutput, calls=%fused_computation.16 | convolution fusion | flops 4299161600 | bytes 13631488 | tf_op jit(solution)/shard_map/dot_general | solution.py:24
  267.0 7.4 %reshape.310 = bf16[128,64,256]{2,1,0:T(8,128)(2,1)} reshape(bf16[512,4096]{1,0:T(8,128)(2,1)} %fusion.12) | data formatting | bytes 8388608 | tf_op jit(solution)/shard_map/reshape | solution.py:86
  274.4 67.7 %all-to-all-done.2 = bf16[128,144,256]{2,1,0:T(8,128)(2,1)} async-done(((bf16[128,144,256]{2,1,0:T(8,128)(2,1)}), bf16[128,144,256]{2,1,0:T(8,128)(2,1)}, u32[]{:S(2)}, u32[]{:S(2)}) %all-to-all-start.2) | async-done | bytes 9437216 | tf_op jit(solution)/shard_map/all_to_all | solution.py:69
  342.1 12.3 %all-to-all-start.3 = ((bf16[128,64,256]{2,1,0:T(8,128)(2,1)}), bf16[128,64,256]{2,1,0:T(8,128)(2,1)}, u32[]{:S(2)}, u32[]{:S(2)}) async-start(bf16[128,64,256]{2,1,0:T(8,128)(2,1)} %reshape.310), calls=%async_computation.3 | async-start | bytes 8388608 | tf_op jit(solution)/shard_map/all_to_all | solution.py:69
  370.2 6.9 %fusion.2 = f32[384,1024]{1,0:T(8,128)S(1)} fusion(bf16[384,4096]{1,0:T(8,128)(2,1)} %reshape.312, bf16[1,4096,1024]{2,1,0:T(8,128)(2,1)} %param.14), kind=kOutput, calls=%fused_computation.6 | convolution fusion | flops 3221225472 | bytes 13107200 | tf_op jit(solution)/shard_map/dot_general | solution.py:13
  379.3 10.4 %fusion.18 = bf16[384,4096]{1,0:T(8,128)(2,1)} fusion(bf16[1,4096,1024]{2,1,0:T(8,128)(2,1)} %param.14, bf16[384,512]{1,0:T(8,128)(2,1)S(1)} %get-tuple-element.40, bf16[384,512]{1,0:T(8,128)(2,1)S(1)} %get-tuple-element.38), kind=kOutput, calls=%fused_computation.18 | convolution fusion | flops 3224371200 | bytes 12320768 | tf_op jit(solution)/shard_map/dot_general | solution.py:24
  424.1 7.4 %reshape.316 = bf16[512,4096]{1,0:T(8,128)(2,1)} reshape(bf16[128,64,256]{2,1,0:T(8,128)(2,1)} %all-to-all-done.3) | data formatting | bytes 8388608 | tf_op jit(solution)/shard_map/reshape | solution.py:104
  437.8 26.8 %all-to-all-done.4 = bf16[128,64,256]{2,1,0:T(8,128)(2,1)} async-done(((bf16[128,64,256]{2,1,0:T(8,128)(2,1)}), bf16[128,64,256]{2,1,0:T(8,128)(2,1)}, u32[]{:S(2)}, u32[]{:S(2)}) %all-to-all-start.4) | async-done | bytes 4194336 | tf_op jit(solution)/shard_map/all_to_all | solution.py:69
  (125 shorter events, 115.6 us)
Async XLA Ops:
  0.6 4.6 copy-start.16
  0.6 4.6 copy-start.8
  1.8 3.8 copy-start.9
  3.2 1.0 copy-start.13
  22.0 87.3 %all-to-all-start = ((bf16[128,96,256]{2,1,0:T(8,128)(2,1)}), bf16[128,96,256]{2,1,0:T(8,128)(2,1)}, u32[]{:S(2)}, u32[]{:S(2)}) async-start(bf16[128,96,256]{2,1,0:T(8,128)(2,1)} %reshape.300), calls=%async_computation | async-start | bytes 12582912 | tf_op jit(solution)/shard_map/all_to_all | solution.py:69
  109.3 105.6 %all-to-all-start.1 = ((bf16[128,128,256]{2,1,0:T(8,128)(2,1)}), bf16[128,128,256]{2,1,0:T(8,128)(2,1)}, u32[]{:S(2)}, u32[]{:S(2)}) async-start(bf16[128,128,256]{2,1,0:T(8,128)(2,1)} %reshape.302), calls=%async_computation.1 | async-start | bytes 16777216 | tf_op jit(solution)/shard_map/all_to_all | solution.py:69
  146.2 6.9 %copy-start.4 = (bf16[384,4096]{1,0:T(8,128)(2,1)S(1)}, bf16[384,4096]{1,0:T(8,128)(2,1)}, u32[]{:S(2)}) copy-start(bf16[384,4096]{1,0:T(8,128)(2,1)} %reshape.303) | copy-start | bytes 9437188
  146.2 6.9 %copy-start.17 = (bf16[1,512,4096]{2,1,0:T(8,128)(2,1)S(1)}, bf16[1,512,4096]{2,1,0:T(8,128)(2,1)}, u32[]{:S(2)}) copy-start(bf16[1,512,4096]{2,1,0:T(8,128)(2,1)} %param.15) | copy-start | bytes 12582916
  214.9 127.2 %all-to-all-start.2 = ((bf16[128,144,256]{2,1,0:T(8,128)(2,1)}), bf16[128,144,256]{2,1,0:T(8,128)(2,1)}, u32[]{:S(2)}, u32[]{:S(2)}) async-start(bf16[128,144,256]{2,1,0:T(8,128)(2,1)} %pad_maximum_fusion), calls=%async_computation.2 | async-start | bytes 18874368 | tf_op jit(solution)/shard_map/all_to_all | solution.py:69
  246.2 8.4 %copy-start.3 = (bf16[512,4096]{1,0:T(8,128)(2,1)S(1)}, bf16[512,4096]{1,0:T(8,128)(2,1)}, u32[]{:S(2)}) copy-start(bf16[512,4096]{1,0:T(8,128)(2,1)} %reshape.308) | copy-start | bytes 12582916
  246.2 8.4 %copy-start.18 = (bf16[1,512,4096]{2,1,0:T(8,128)(2,1)S(1)}, bf16[1,512,4096]{2,1,0:T(8,128)(2,1)}, u32[]{:S(2)}) copy-start(bf16[1,512,4096]{2,1,0:T(8,128)(2,1)} %param.15) | copy-start | bytes 12582916
  342.1 64.4 %all-to-all-start.3 = ((bf16[128,64,256]{2,1,0:T(8,128)(2,1)}), bf16[128,64,256]{2,1,0:T(8,128)(2,1)}, u32[]{:S(2)}, u32[]{:S(2)}) async-start(bf16[128,64,256]{2,1,0:T(8,128)(2,1)} %reshape.310), calls=%async_computation.3 | async-start | bytes 8388608 | tf_op jit(solution)/shard_map/all_to_all | solution.py:69
  370.2 6.9 %copy-start.5 = (bf16[384,4096]{1,0:T(8,128)(2,1)S(1)}, bf16[384,4096]{1,0:T(8,128)(2,1)}, u32[]{:S(2)}) copy-start(bf16[384,4096]{1,0:T(8,128)(2,1)} %reshape.311) | copy-start | bytes 9437188
  370.2 6.9 %copy-start.19 = (bf16[1,512,4096]{2,1,0:T(8,128)(2,1)S(1)}, bf16[1,512,4096]{2,1,0:T(8,128)(2,1)}, u32[]{:S(2)}) copy-start(bf16[1,512,4096]{2,1,0:T(8,128)(2,1)} %param.15) | copy-start | bytes 12582916
  401.7 10.7 %copy-start.11 = (s32[1024]{0:T(1024)S(1)}, s32[1024]{0:T(1024)}, u32[]{:S(2)}) copy-start(s32[1024]{0:T(1024)} %copy-done.10) | copy-start | bytes 12292
  401.7 10.8 %copy-start.12 = (s32[128,8]{0,1:T(8,128)S(1)}, s32[128,8]{0,1:T(8,128)}, u32[]{:S(2)}) copy-start(s32[128,8]{0,1:T(8,128)} %param.11) | copy-start | bytes 12292
  401.7 11.0 %copy-start.15 = (f32[128,8]{0,1:T(8,128)S(1)}, f32[128,8]{0,1:T(8,128)}, u32[]{:S(2)}) copy-start(f32[128,8]{0,1:T(8,128)} %param.10) | copy-start | bytes 12292
  406.5 58.0 %all-to-all-start.4 = ((bf16[128,64,256]{2,1,0:T(8,128)(2,1)}), bf16[128,64,256]{2,1,0:T(8,128)(2,1)}, u32[]{:S(2)}, u32[]{:S(2)}) async-start(bf16[128,64,256]{2,1,0:T(8,128)(2,1)} %pad_maximum_fusion.1), calls=%async_computation.4 | async-start | bytes 8388608 | tf_op jit(solution)/shard_map/all_to_all | solution.py:69
  420.3 1.7 copy-start.7
  431.5 3.4 copy-start
  431.5 4.1 copy-start.1
  470.6 6.1 %copy-start.14 = (s32[1024]{0:T(1024)S(1)}, s32[1024]{0:T(1024)}, u32[]{:S(2)}) copy-start(s32[1024]{0:T(1024)} %copy-done.13) | copy-start | bytes 12292
  470.6 7.6 %copy-start.6 = (f32[128,384]{1,0:T(8,128)S(1)}, f32[128,384]{1,0:T(8,128)}, u32[]{:S(2)}) copy-start(f32[128,384]{1,0:T(8,128)} %select_reduce_fusion.3) | copy-start | bytes 589828
  478.3 1.6 copy-start.2
  (1 other events, 0.6 us)
